TPU v7x, 32 devices: a whole 2x2x4 slice. The times are simulated.
32 devices in a mesh: groups: 2 (over y), frames: 4 (over z), heads: 4 (over x, core).
Axes of the slice: x: 2, y: 2, z: 4, core: 2. Of those that a mesh axis runs over, the one named last changes fastest.
Arguments:
- query_heads: bfloat16 [16384, 896], P(('groups', 'frames'), 'heads'), parts along dimension 0, may hold values from -6 to 6
- key_heads: bfloat16 [16384, 896], P(('groups', 'frames'), 'heads'), parts along dimension 0, may hold values from -0.04 to 8
- value_heads: bfloat16 [16384, 896], P(('groups', 'frames'), 'heads'), parts along dimension 0, may hold values from -6 to 6
- residual: bfloat16 [16384, 2240], P(('groups', 'frames', 'heads')), parts along dimension 0, may hold values from -6 to 6
- out_proj: bfloat16 [896, 2240], P('frames'), may hold values from -0.1875 to 0.1875
- frame_gate: float32 [32, 2240], P(('groups', 'frames')), parts along dimension 0, may hold values from -4 to 4
Outputs:
- updated: bfloat16 [16384, 2240], P(('groups', 'frames', 'heads')), parts along dimension 0
There are 2 independent parts, one for each index of `groups`. A program takes and returns all parts, laid end to end along the dimension named above; an argument that names none is the same for every part. Nothing has to cross between parts.
All inputs are finite; a program needn't handle non-finite values.
Results may differ from a plain program's by a relative error of at most 0.0033.
Values may be sent and summed in bfloat16 or wider, within the bound.
No kernel may reach another device: no remote copies, remote signals or barrier semaphores. Data moves between devices by JAX's collectives and lax.ppermute only.
A program may use at most 64 MiB of HBM per device.

v0:
```python
import jax
import jax.numpy as jnp
from jax import lax
from jax.sharding import PartitionSpec as P

HD = 112
FRAME_TOK = 512


EPSILON = 1e-06


def _exclusive_prefix(x, nf):
    if nf <= 8:
        total = jnp.zeros_like(x)
        for d in range(1, nf):
            total = total + lax.ppermute(x, "frames", [(i, i + d) for i in range(nf - d)])
        return total
    y = lax.ppermute(x, "frames", [(i, i + 1) for i in range(nf - 1)])
    covered = 1
    while covered < nf - 1:
        y = y + lax.ppermute(y, "frames", [(i, i + covered) for i in range(nf - covered)])
        covered *= 2
    return y


def _ring_out_proj(out_proj, nf, nh, ng):
    rows, _ = out_proj.shape
    sub = rows // (2 * ng)
    g = lax.axis_index("groups")
    core = lax.axis_index("heads") % 2
    shares = [jnp.remainder(g - s, ng) * 2 + core for s in range(ng)]
    shares += [jnp.remainder(g - s, ng) * 2 + 1 - core for s in range(ng)]
    pieces = [lax.dynamic_slice_in_dim(out_proj, share * sub, sub, axis=0) for share in shares]
    ring = [(i, (i + 1) % nf) for i in range(nf)]
    swap = [(a, a ^ 1) for a in range(nh)]
    piece = pieces[0]
    for _ in range(1, nf):
        piece = lax.ppermute(piece, "frames", ring)
        from_groups = [piece] + [
            lax.ppermute(piece, "groups", [(a, (a + s) % ng) for a in range(ng)])
            for s in range(1, ng)
        ]
        from_core = lax.ppermute(jnp.stack(from_groups), "heads", swap)
        pieces += from_groups + [from_core[s] for s in range(ng)]
    return jnp.concatenate(pieces, axis=0), jnp.stack(shares)


def make_per_device(nf, nh, ng):
    def per_device(query_heads, key_heads, value_heads, residual, out_proj, frame_gate):
        weights, shares = _ring_out_proj(out_proj, nf, nh, ng)
        attended = _attend(query_heads, key_heads, value_heads, nf)
        return _project(attended, weights, shares, residual, frame_gate, nf, ng)

    return per_device


def _attend(query_heads, key_heads, value_heads, nf):
    length, width = query_heads.shape
    frames_here = length // FRAME_TOK
    heads_here = width // HD
    block_shape = (frames_here, FRAME_TOK, width)
    query_pos = jnp.maximum(query_heads, 0).reshape(block_shape)
    key_pos = jnp.maximum(key_heads, 0).reshape(block_shape)
    value_frames = value_heads.reshape(block_shape)
    lane_head = jnp.arange(width, dtype=jnp.int32) // HD
    same_head = lane_head[:, None] == lane_head[None, :]

    frame_state = jnp.einsum(
        "fti,ftj->fij", key_pos, value_frames, preferred_element_type=jnp.float32
    )
    frame_state = jnp.where(same_head[None], frame_state, 0.0)
    frame_sum = jnp.sum(key_pos, axis=1, dtype=jnp.float32)
    own_state = jnp.sum(frame_state, axis=0)
    own_sum = jnp.sum(frame_sum, axis=0)

    blocks = [
        own_state[a * HD:(a + 1) * HD, a * HD:(a + 1) * HD] for a in range(heads_here)
    ]
    compact = jnp.concatenate(
        [jnp.stack(blocks), own_sum.reshape(heads_here, 1, HD)], axis=1
    )
    earlier = _exclusive_prefix(compact, nf)
    eye = jnp.eye(heads_here, dtype=jnp.float32)
    earlier_state = jnp.einsum(
        "aij,ab->aibj", earlier[:, :HD, :], eye, precision=lax.Precision.HIGHEST
    ).reshape(width, width)
    earlier_sum = earlier[:, HD, :].reshape(width)

    prefix_state = earlier_state[None] + jnp.cumsum(frame_state, axis=0)
    prefix_sum = earlier_sum[None] + jnp.cumsum(frame_sum, axis=0)
    state_round = prefix_state.astype(jnp.bfloat16)
    sum_round = prefix_sum.astype(jnp.bfloat16)
    sum_matrix = jnp.where(same_head[None], sum_round[:, :, None], jnp.zeros((), jnp.bfloat16))
    numerator = jnp.einsum(
        "fti,fij->ftj", query_pos, state_round, preferred_element_type=jnp.float32
    )
    denominator = (
        jnp.einsum("fti,fij->ftj", query_pos, sum_matrix, preferred_element_type=jnp.float32)
        + EPSILON
    )
    return (numerator / denominator).astype(jnp.bfloat16).reshape(length, width)


def _project(attended, weights, shares, residual, frame_gate, nf, ng):
    rows_here = residual.shape[0]
    head_pos = lax.axis_index("heads")
    if rows_here <= FRAME_TOK and FRAME_TOK % rows_here == 0:
        gate_rows = lax.dynamic_slice_in_dim(
            frame_gate, (head_pos * rows_here) // FRAME_TOK, 1, axis=0
        )
    else:
        row_frame = (head_pos * rows_here + jnp.arange(rows_here, dtype=jnp.int32)) // FRAME_TOK
        gate_rows = jnp.take(frame_gate, row_frame, axis=0)
    token_rows = lax.all_to_all(attended, "heads", split_axis=0, concat_axis=1, tiled=True)
    nparts = 2 * ng
    depth = weights.shape[0]
    sub = depth // (nf * nparts)
    j = lax.axis_index("frames")
    block = jnp.remainder(j - jnp.arange(nf, dtype=jnp.int32), nf)
    order = (block[:, None] * nparts + shares[None, :]).reshape(-1)
    source = (order[:, None] * sub + jnp.arange(sub, dtype=jnp.int32)[None, :]).reshape(-1)
    pick = (jnp.arange(depth, dtype=jnp.int32)[:, None] == source[None, :]).astype(jnp.bfloat16)
    matched = jnp.dot(token_rows, pick, preferred_element_type=jnp.float32).astype(jnp.bfloat16)
    projected = jnp.dot(matched, weights, preferred_element_type=jnp.float32)
    return (residual.astype(jnp.float32) + gate_rows * projected).astype(jnp.bfloat16)


def solution(mesh):
    nf = mesh.shape["frames"]
    nh = mesh.shape["heads"]
    ng = mesh.shape["groups"]
    in_specs = (
        P(("groups", "frames"), "heads"),
        P(("groups", "frames"), "heads"),
        P(("groups", "frames"), "heads"),
        P(("groups", "frames", "heads"), None),
        P("frames", None),
        P(("groups", "frames"), None),
    )
    out_specs = P(("groups", "frames", "heads"), None)
    return jax.shard_map(
        make_per_device(nf, nh, ng), mesh=mesh, in_specs=in_specs, out_specs=out_specs,
        check_vma=False,
    )
```

profile of v0, /device:TPU:0, one launch (start us, length us, event | category | flops | bytes accessed | tf_op | source)
XLA Modules:
  0.0 75.4 jit_solution(6916735546781286356)
XLA Ops:
  0.0 1.3 %broadcast_maximum_fusion = bf16[2048,224]{0,1:T(8,128)(2,1)S(1)} fusion(bf16[2048,224]{0,1:T(8,128)(2,1)} %param.7), kind=kLoop, calls=%fused_computation.26 | loop fusion | flops 458752 | bytes 1835008 | tf_op jit(solution)/shard_map/max | solution.py:64
  1.3 1.4 %convert_reduce_fusion.1 = f32[224]{0:T(256)S(1)} fusion(bf16[2048,224]{0,1:T(8,128)(2,1)} %param.7), kind=kLoop, calls=%fused_computation.7 | loop fusion | flops 1376032 | bytes 918400 | tf_op jit(solution)/shard_map/reduce_sum | solution.py:75
  2.9 2.6 %fusion.28 = (f32[224,224]{1,0:T(8,128)S(1)}, f32[4,224,224]{2,1,0:T(8,128)}) fusion(bf16[28,4,8,512]{3,2,1,0:T(8,128)(2,1)} %bitcast.77, bf16[28,4,8,512]{3,2,1,0:T(8,128)(2,1)S(1)} %bitcast.67, pred[224,224]{1,0:T(8,128)(4,1)S(1)} %broadcast_compare_fusion), kind=kOutput, calls=%fused_computation.77 | convolution fusion | flops 205872128 | bytes 2888704 | tf_op jit(solution)/shard_map/fti,ftj->fij/dot_general | solution.py:69
  6.3 5.6 %collective-permute-start = (f32[2,113,112]{2,1,0:T(8,128)}, f32[2,113,112]{2,1,0:T(8,128)}, u32[]{:S(2)}, u32[]{:S(2)}) collective-permute-start(f32[2,113,112]{2,1,0:T(8,128)} %pad_maximum_fusion.3), channel_id=1, source_target_pairs={{0,4},{4,8},{8,12},{1,5},{5,9},{9,13},{2,6},{6,10},{10,14},{3,7},{... | collective-permute-start | bytes 303752 | tf_op jit(solution)/shard_map/ppermute | solution.py:17
  11.9 4.5 %collective-permute-start.1 = (f32[2,113,112]{2,1,0:T(8,128)}, f32[2,113,112]{2,1,0:T(8,128)}, u32[]{:S(2)}, u32[]{:S(2)}) collective-permute-start(f32[2,113,112]{2,1,0:T(8,128)} %pad_maximum_fusion.3), channel_id=1, source_target_pairs={{0,8},{4,12},{1,9},{5,13},{2,10},{6,14},{3,11},{7,15},{16,24},{20,... | collective-permute-start | bytes 303752 | tf_op jit(solution)/shard_map/ppermute | solution.py:17
  16.4 1.9 %collective-permute-start.2 = (f32[2,113,112]{2,1,0:T(8,128)}, f32[2,113,112]{2,1,0:T(8,128)}, u32[]{:S(2)}, u32[]{:S(2)}) collective-permute-start(f32[2,113,112]{2,1,0:T(8,128)} %pad_maximum_fusion.3), channel_id=1, source_target_pairs={{0,12},{1,13},{2,14},{3,15},{16,28},{17,29},{18,30},{19,31}} | collective-permute-start | bytes 303752 | tf_op jit(solution)/shard_map/ppermute | solution.py:17
  18.4 0.7 constant_dynamic-update-slice_fusion.6
  20.2 1.2 %broadcast_maximum_fusion.1 = bf16[2048,224]{0,1:T(8,128)(2,1)S(1)} fusion(bf16[2048,224]{0,1:T(8,128)(2,1)} %param.6), kind=kLoop, calls=%fused_computation.27 | loop fusion | flops 458752 | bytes 1835008 | tf_op jit(solution)/shard_map/max | solution.py:63
  21.9 0.7 dynamic-slice_dynamic-update-slice_fusion.2
  23.3 0.7 dynamic-slice_dynamic-update-slice_fusion
  24.3 1.0 %add_add_fusion = f32[2,113,112]{2,1,0:T(8,128)S(1)} fusion(f32[2,113,112]{2,1,0:T(8,128)} %collective-permute-done.2, f32[2,113,112]{2,1,0:T(8,128)} %collective-permute-done, f32[2,113,112]{2,1,0:T(8,128)} %collective-permute-done.1), kind=kLoop, calls=%fused_computation.48 | loop fusion | flops 50624 | bytes 404992 | tf_op jit(solution)/shard_map/add | solution.py:17
  26.6 1.6 %divide_convert_fusion = bf16[4,512,224]{1,2,0:T(8,128)(2,1)} fusion(f32[4,512,224]{1,2,0:T(8,128)S(1)} %fusion.11, bf16[28,4,8,512]{3,2,1,0:T(8,128)(2,1)S(1)} %bitcast.69, pred[224,224]{1,0:T(8,128)(4,1)S(1)} %copy-done.4, bf16[4,224]{1,0:T(4,128)(2,1)S(1)} %copy.17), kind=kOutput, calls=%fused_computation.5 | convolution fusion | flops 207097856 | bytes 3721984 | tf_op jit(solution)/shard_map/fti,fij->ftj/dot_general | solution.py:99
  28.2 3.5 %all-to-all-start = ((bf16[4,512,224]{1,2,0:T(8,128)(2,1)}), bf16[4,512,224]{1,2,0:T(8,128)(2,1)S(1)}, u32[]{:S(2)}, u32[]{:S(2)}) async-start(bf16[4,512,224]{1,2,0:T(8,128)(2,1)} %divide_convert_fusion), calls=%async_computation | async-start | bytes 1835008 | tf_op jit(solution)/shard_map/all_to_all | solution.py:115
  31.8 1.6 %collective-permute-start.4 = (bf16[56,2240]{1,0:T(8,128)(2,1)S(1)}, bf16[56,2240]{1,0:T(8,128)(2,1)S(1)}, u32[]{:S(2)}, u32[]{:S(2)}) collective-permute-start(bf16[56,2240]{1,0:T(8,128)(2,1)S(1)} %collective-permute-done.3), channel_id=1, source_target_pairs={{0,16},{16,0},{1,17},{17,1},{2,18},{18,2},{3,19},{19,3},{4,20},{20... | collective-permute-start | bytes 752648 | tf_op jit(solution)/shard_map/ppermute | solution.py:41
  33.6 0.7 constant_dynamic-update-slice_fusion.5
  34.3 6.0 %collective-permute-done.4 = bf16[56,2240]{1,0:T(8,128)(2,1)S(1)} collective-permute-done((bf16[56,2240]{1,0:T(8,128)(2,1)S(1)}, bf16[56,2240]{1,0:T(8,128)(2,1)S(1)}, u32[]{:S(2)}, u32[]{:S(2)}) %collective-permute-start.4) | collective-permute-done | bytes 250912 | tf_op jit(solution)/shard_map/ppermute | solution.py:41
  40.5 3.2 %collective-permute-done.6 = bf16[56,2240]{1,0:T(8,128)(2,1)S(1)} collective-permute-done((bf16[56,2240]{1,0:T(8,128)(2,1)S(1)}, bf16[56,2240]{1,0:T(8,128)(2,1)S(1)}, u32[]{:S(2)}, u32[]{:S(2)}) %collective-permute-start.6) | collective-permute-done | bytes 250912 | tf_op jit(solution)/shard_map/ppermute | solution.py:39
  44.2 0.7 constant_dynamic-update-slice_fusion.4
  44.9 8.4 %collective-permute-done.9 = bf16[56,2240]{1,0:T(8,128)(2,1)S(1)} collective-permute-done((bf16[56,2240]{1,0:T(8,128)(2,1)S(1)}, bf16[56,2240]{1,0:T(8,128)(2,1)S(1)}, u32[]{:S(2)}, u32[]{:S(2)}) %collective-permute-start.9) | collective-permute-done | bytes 250912 | tf_op jit(solution)/shard_map/ppermute | solution.py:39
  53.3 1.5 %collective-permute-start.10 = (bf16[56,2240]{1,0:T(8,128)(2,1)S(1)}, bf16[56,2240]{1,0:T(8,128)(2,1)S(1)}, u32[]{:S(2)}, u32[]{:S(2)}) collective-permute-start(bf16[56,2240]{1,0:T(8,128)(2,1)S(1)} %collective-permute-done.9), channel_id=1, source_target_pairs={{0,16},{16,0},{1,17},{17,1},{2,18},{18,2},{3,19},{19,3},{4,20},{20... | collective-permute-start | bytes 752648 | tf_op jit(solution)/shard_map/ppermute | solution.py:41
  55.0 4.9 %collective-permute-done.10 = bf16[56,2240]{1,0:T(8,128)(2,1)S(1)} collective-permute-done((bf16[56,2240]{1,0:T(8,128)(2,1)S(1)}, bf16[56,2240]{1,0:T(8,128)(2,1)S(1)}, u32[]{:S(2)}, u32[]{:S(2)}) %collective-permute-start.10) | collective-permute-done | bytes 250912 | tf_op jit(solution)/shard_map/ppermute | solution.py:41
  60.0 0.7 fusion.22
  60.7 0.7 fusion.21
  61.5 0.8 %constant_dynamic-update-slice_fusion.3 = bf16[896,2240]{1,0:T(8,128)(2,1)} fusion(bf16[896,2240]{1,0:T(8,128)(2,1)} %fusion.21, bf16[56,2240]{1,0:T(8,128)(2,1)S(1)} %collective-permute-done.6), kind=kLoop, calls=%fused_computation.56 | loop fusion | bytes 508928
  62.2 0.7 constant_dynamic-update-slice_fusion.2
  62.9 0.7 fusion.20
  63.7 0.7 fusion.19
  64.4 0.7 constant_dynamic-update-slice_fusion.1
  65.1 0.7 constant_dynamic-update-slice_fusion
  65.9 0.7 fusion.18
  66.6 0.7 fusion.17
  67.3 8.1 %fusion.1 = bf16[512,2240]{0,1:T(8,128)(2,1)} fusion(bf16[896,2240]{1,0:T(8,128)(2,1)} %fusion.17, bf16[512,2240]{0,1:T(8,128)(2,1)} %param.9, f32[2240]{0:T(1024)S(1)} %dynamic-slice_reduce_fusion, bf16[512,896]{0,1:T(8,128)(2,1)S(1)} %bitcast.76, s32[896]{0:T(1024)S(1)} %add.163), kind=kOutput, calls=%fused_computation.2 | convolution fusion | flops 2883141632 | bytes 9531648 | tf_op jit(solution)/shard_map/dot_general | solution.py:125
  (54 shorter events, 5.7 us)
Async XLA Ops:
  0.0 24.0 %copy-start = (f32[4,2240]{1,0:T(4,128)S(1)}, f32[4,2240]{1,0:T(4,128)}, u32[]{:S(2)}) copy-start(f32[4,2240]{1,0:T(4,128)} %param.11) | copy-start | bytes 107524
  0.0 18.4 %copy-start.1 = (bf16[224,2240]{1,0:T(8,128)(2,1)S(1)}, bf16[224,2240]{1,0:T(8,128)(2,1)}, u32[]{:S(2)}) copy-start(bf16[224,2240]{1,0:T(8,128)(2,1)} %param.10) | copy-start | bytes 3010564
  2.9 2.6 %copy-start.3 = (pred[224,224]{1,0:T(8,128)(4,1)}, pred[224,224]{1,0:T(8,128)(4,1)S(1)}, u32[]{:S(2)}) copy-start(pred[224,224]{1,0:T(8,128)(4,1)S(1)} %broadcast_compare_fusion) | copy-start | bytes 150532
  6.3 18.0 %collective-permute-start = (f32[2,113,112]{2,1,0:T(8,128)}, f32[2,113,112]{2,1,0:T(8,128)}, u32[]{:S(2)}, u32[]{:S(2)}) collective-permute-start(f32[2,113,112]{2,1,0:T(8,128)} %pad_maximum_fusion.3), channel_id=1, source_target_pairs={{0,4},{4,8},{8,12},{1,5},{5,9},{9,13},{2,6},{6,10},{10,14},{3,7},{... | collective-permute-start | bytes 303752 | tf_op jit(solution)/shard_map/ppermute | solution.py:17
  11.9 12.4 %collective-permute-start.1 = (f32[2,113,112]{2,1,0:T(8,128)}, f32[2,113,112]{2,1,0:T(8,128)}, u32[]{:S(2)}, u32[]{:S(2)}) collective-permute-start(f32[2,113,112]{2,1,0:T(8,128)} %pad_maximum_fusion.3), channel_id=1, source_target_pairs={{0,8},{4,12},{1,9},{5,13},{2,10},{6,14},{3,11},{7,15},{16,24},{20,... | collective-permute-start | bytes 303752 | tf_op jit(solution)/shard_map/ppermute | solution.py:17
  16.4 7.9 %collective-permute-start.2 = (f32[2,113,112]{2,1,0:T(8,128)}, f32[2,113,112]{2,1,0:T(8,128)}, u32[]{:S(2)}, u32[]{:S(2)}) collective-permute-start(f32[2,113,112]{2,1,0:T(8,128)} %pad_maximum_fusion.3), channel_id=1, source_target_pairs={{0,12},{1,13},{2,14},{3,15},{16,28},{17,29},{18,30},{19,31}} | collective-permute-start | bytes 303752 | tf_op jit(solution)/shard_map/ppermute | solution.py:17
  19.1 12.7 %collective-permute-start.3 = (bf16[56,2240]{1,0:T(8,128)(2,1)S(1)}, bf16[56,2240]{1,0:T(8,128)(2,1)S(1)}, u32[]{:S(2)}, u32[]{:S(2)}) collective-permute-start(bf16[56,2240]{1,0:T(8,128)(2,1)S(1)} %get-tuple-element.6), channel_id=1, source_target_pairs={{0,4},{4,8},{8,12},{12,0},{1,5},{5,9},{9,13},{13,1},{2,6},{6,10},{... | collective-permute-start | bytes 752648 | tf_op jit(solution)/shard_map/ppermute | solution.py:39
  21.9 4.1 %copy-start.2 = (f32[4,224,224]{2,1,0:T(8,128)S(1)}, f32[4,224,224]{2,1,0:T(8,128)}, u32[]{:S(2)}) copy-start(f32[4,224,224]{2,1,0:T(8,128)} %get-tuple-element.10) | copy-start | bytes 2408452
  24.0 2.6 %copy-start.4 = (pred[224,224]{1,0:T(8,128)(4,1)S(1)}, pred[224,224]{1,0:T(8,128)(4,1)}, u32[]{:S(2)}) copy-start(pred[224,224]{1,0:T(8,128)(4,1)} %copy-done.3) | copy-start | bytes 150532
  28.2 39.1 %all-to-all-start = ((bf16[4,512,224]{1,2,0:T(8,128)(2,1)}), bf16[4,512,224]{1,2,0:T(8,128)(2,1)S(1)}, u32[]{:S(2)}, u32[]{:S(2)}) async-start(bf16[4,512,224]{1,2,0:T(8,128)(2,1)} %divide_convert_fusion), calls=%async_computation | async-start | bytes 1835008 | tf_op jit(solution)/shard_map/all_to_all | solution.py:115
  31.8 8.6 %collective-permute-start.4 = (bf16[56,2240]{1,0:T(8,128)(2,1)S(1)}, bf16[56,2240]{1,0:T(8,128)(2,1)S(1)}, u32[]{:S(2)}, u32[]{:S(2)}) collective-permute-start(bf16[56,2240]{1,0:T(8,128)(2,1)S(1)} %collective-permute-done.3), channel_id=1, source_target_pairs={{0,16},{16,0},{1,17},{17,1},{2,18},{18,2},{3,19},{19,3},{4,20},{20... | collective-permute-start | bytes 752648 | tf_op jit(solution)/shard_map/ppermute | solution.py:41
  33.3 10.3 %collective-permute-start.6 = (bf16[56,2240]{1,0:T(8,128)(2,1)S(1)}, bf16[56,2240]{1,0:T(8,128)(2,1)S(1)}, u32[]{:S(2)}, u32[]{:S(2)}) collective-permute-start(bf16[56,2240]{1,0:T(8,128)(2,1)S(1)} %collective-permute-done.3), channel_id=1, source_target_pairs={{0,4},{4,8},{8,12},{12,0},{1,5},{5,9},{9,13},{13,1},{2,6},{6,10},{... | collective-permute-start | bytes 752648 | tf_op jit(solution)/shard_map/ppermute | solution.py:39
  40.4 19.6 %collective-permute-start.5 = (bf16[2,56,2240]{2,1,0:T(8,128)(2,1)S(1)}, bf16[2,56,2240]{2,1,0:T(8,128)(2,1)S(1)}, u32[]{:S(2)}, u32[]{:S(2)}) collective-permute-start(bf16[2,56,2240]{2,1,0:T(8,128)(2,1)S(1)} %pad_maximum_fusion), channel_id=1, source_target_pairs={{0,1},{1,0},{2,3},{3,2},{4,5},{5,4},{6,7},{7,6},{8,9},{9,8},{10,11... | collective-permute-start | bytes 1505288 | tf_op jit(solution)/shard_map/ppermute | solution.py:44
  43.7 11.2 %collective-permute-start.7 = (bf16[56,2240]{1,0:T(8,128)(2,1)S(1)}, bf16[56,2240]{1,0:T(8,128)(2,1)S(1)}, u32[]{:S(2)}, u32[]{:S(2)}) collective-permute-start(bf16[56,2240]{1,0:T(8,128)(2,1)S(1)} %collective-permute-done.6), channel_id=1, source_target_pairs={{0,16},{16,0},{1,17},{17,1},{2,18},{18,2},{3,19},{19,3},{4,20},{20... | collective-permute-start | bytes 752648 | tf_op jit(solution)/shard_map/ppermute | solution.py:41
  44.2 9.2 %collective-permute-start.9 = (bf16[56,2240]{1,0:T(8,128)(2,1)S(1)}, bf16[56,2240]{1,0:T(8,128)(2,1)S(1)}, u32[]{:S(2)}, u32[]{:S(2)}) collective-permute-start(bf16[56,2240]{1,0:T(8,128)(2,1)S(1)} %collective-permute-done.6), channel_id=1, source_target_pairs={{0,4},{4,8},{8,12},{12,0},{1,5},{5,9},{9,13},{13,1},{2,6},{6,10},{... | collective-permute-start | bytes 752648 | tf_op jit(solution)/shard_map/ppermute | solution.py:39
  53.3 6.5 %collective-permute-start.10 = (bf16[56,2240]{1,0:T(8,128)(2,1)S(1)}, bf16[56,2240]{1,0:T(8,128)(2,1)S(1)}, u32[]{:S(2)}, u32[]{:S(2)}) collective-permute-start(bf16[56,2240]{1,0:T(8,128)(2,1)S(1)} %collective-permute-done.9), channel_id=1, source_target_pairs={{0,16},{16,0},{1,17},{17,1},{2,18},{18,2},{3,19},{19,3},{4,20},{20... | collective-permute-start | bytes 752648 | tf_op jit(solution)/shard_map/ppermute | solution.py:41
  54.9 8.0 %collective-permute-start.8 = (bf16[2,56,2240]{2,1,0:T(8,128)(2,1)S(1)}, bf16[2,56,2240]{2,1,0:T(8,128)(2,1)S(1)}, u32[]{:S(2)}, u32[]{:S(2)}) collective-permute-start(bf16[2,56,2240]{2,1,0:T(8,128)(2,1)S(1)} %pad_maximum_fusion.1), channel_id=1, source_target_pairs={{0,1},{1,0},{2,3},{3,2},{4,5},{5,4},{6,7},{7,6},{8,9},{9,8},{10,11... | collective-permute-start | bytes 1505288 | tf_op jit(solution)/shard_map/ppermute | solution.py:44
  59.9 5.9 %collective-permute-start.11 = (bf16[2,56,2240]{2,1,0:T(8,128)(2,1)S(1)}, bf16[2,56,2240]{2,1,0:T(8,128)(2,1)S(1)}, u32[]{:S(2)}, u32[]{:S(2)}) collective-permute-start(bf16[2,56,2240]{2,1,0:T(8,128)(2,1)S(1)} %pad_maximum_fusion.2), channel_id=1, source_target_pairs={{0,1},{1,0},{2,3},{3,2},{4,5},{5,4},{6,7},{7,6},{8,9},{9,8},{10,11... | collective-permute-start | bytes 1505288 | tf_op jit(solution)/shard_map/ppermute | solution.py:44
where the time goes:
time: 75.8 us; the launch traced here: 75.4 us
  waiting for transfers between devices  22.6 us (30%)
  starting transfers between devices  19.6 us (26%)
  local copies, waits for them, and re-layouts  13 us (17%)
  matrix products  12.8 us (17%)
  other arithmetic  7.16 us (9%)
    ppermute x3, starting transfers between devices, _exclusive_prefix(): lax.ppermute(x, 'frames', [(i, i + d) for i in range(nf - d)])  12 us
    ppermute x3, waiting for transfers between devices, _ring_out_proj(): piece = lax.ppermute(piece, 'frames', ring)  11.6 us
    ppermute x3, waiting for transfers between devices, _ring_out_proj(): lax.ppermute(piece, 'groups', [(a, (a + s) % ng) for a in range(ng)])  10.9 us
    unnamed x25, local copies, waits for them, and re-layouts  10.9 us
    dot_general x1, matrix products, _project(): projected = jnp.dot(matched, weights, preferred_element_type=jnp.float32)  8.08 us
    ppermute x3, starting transfers between devices, _ring_out_proj(): lax.ppermute(piece, 'groups', [(a, (a + s) % ng) for a in range(ng)])  3.61 us
    all_to_all x1, starting transfers between devices, _project(): lax.all_to_all(attended, 'heads', split_axis=0, concat_axis=1, tiled=True)  3.51 us
    dot_general x1, matrix products, _attend(): jnp.einsum('fti,ftj->fij', key_pos, value_frames, preferred_element_type=...  2.58 us
  transfers between devices with their start and end apart: 13, of which 4 were waited for; matrix products, arithmetic and copies ran while one was open for 25% of the time, Pallas kernels for 0%

commit v1 on v0

--- a/solution.py
+++ b/solution.py
@@ -32,25 +32,40 @@
     shares = [jnp.remainder(g - s, ng) * 2 + core for s in range(ng)]
     shares += [jnp.remainder(g - s, ng) * 2 + 1 - core for s in range(ng)]
     pieces = [lax.dynamic_slice_in_dim(out_proj, share * sub, sub, axis=0) for share in shares]
-    ring = [(i, (i + 1) % nf) for i in range(nf)]
+    forward = [(i, (i + 1) % nf) for i in range(nf)]
+    backward = [(i, (i - 1) % nf) for i in range(nf)]
     swap = [(a, a ^ 1) for a in range(nh)]
-    piece = pieces[0]
-    for _ in range(1, nf):
-        piece = lax.ppermute(piece, "frames", ring)
+    offsets = [0]
+
+    def spread(piece):
         from_groups = [piece] + [
             lax.ppermute(piece, "groups", [(a, (a + s) % ng) for a in range(ng)])
             for s in range(1, ng)
         ]
         from_core = lax.ppermute(jnp.stack(from_groups), "heads", swap)
-        pieces += from_groups + [from_core[s] for s in range(ng)]
-    return jnp.concatenate(pieces, axis=0), jnp.stack(shares)
+        return from_groups + [from_core[s] for s in range(ng)]
+
+    ahead = nf // 2
+    behind = nf - 1 - ahead
+    piece_a = pieces[0]
+    piece_b = pieces[0]
+    for t in range(1, ahead + 1):
+        piece_a = lax.ppermute(piece_a, "frames", forward)
+        if t <= behind:
+            piece_b = lax.ppermute(piece_b, "frames", backward)
+        pieces += spread(piece_a)
+        offsets.append(-t)
+        if t <= behind:
+            pieces += spread(piece_b)
+            offsets.append(t)
+    return jnp.concatenate(pieces, axis=0), jnp.stack(shares), offsets
 
 
 def make_per_device(nf, nh, ng):
     def per_device(query_heads, key_heads, value_heads, residual, out_proj, frame_gate):
-        weights, shares = _ring_out_proj(out_proj, nf, nh, ng)
+        weights, shares, offsets = _ring_out_proj(out_proj, nf, nh, ng)
         attended = _attend(query_heads, key_heads, value_heads, nf)
-        return _project(attended, weights, shares, residual, frame_gate, nf, ng)
+        return _project(attended, weights, shares, offsets, residual, frame_gate, nf, ng)
 
     return per_device
 
@@ -102,7 +117,7 @@
     return (numerator / denominator).astype(jnp.bfloat16).reshape(length, width)
 
 
-def _project(attended, weights, shares, residual, frame_gate, nf, ng):
+def _project(attended, weights, shares, offsets, residual, frame_gate, nf, ng):
     rows_here = residual.shape[0]
     head_pos = lax.axis_index("heads")
     if rows_here <= FRAME_TOK and FRAME_TOK % rows_here == 0:
@@ -117,7 +132,7 @@
     depth = weights.shape[0]
     sub = depth // (nf * nparts)
     j = lax.axis_index("frames")
-    block = jnp.remainder(j - jnp.arange(nf, dtype=jnp.int32), nf)
+    block = jnp.remainder(j + jnp.array(offsets, dtype=jnp.int32), nf)
     order = (block[:, None] * nparts + shares[None, :]).reshape(-1)
     source = (order[:, None] * sub + jnp.arange(sub, dtype=jnp.int32)[None, :]).reshape(-1)
     pick = (jnp.arange(depth, dtype=jnp.int32)[:, None] == source[None, :]).astype(jnp.bfloat16)

time: 75.8 us -> 73.6 us (0.971)
  waiting for transfers between devices: 22.6 us -> 16.6 us
  starting transfers between devices: 19.6 us -> 22.3 us
  local copies, waits for them, and re-layouts: 13 us -> 14 us
    ppermute x9, waiting for transfers between devices: 22.6 us -> 16.6 us  [the longest x3 16.6 us: spread(): lax.ppermute(piece, 'groups', [(a, (a + s) % ng) for a in range(ng)])]
    ppermute x9, starting transfers between devices: 4.05 us -> 9.81 us  [the longest x2 3.9 us: _ring_out_proj(): piece_a = lax.ppermute(piece_a, 'frames', forward)]
    ppermute x3, starting transfers between devices: 12 us -> 8.99 us  [_exclusive_prefix(): lax.ppermute(x, 'frames', [(i, i + d) for i in range(nf - d)])]
    unnamed x25 -> x27, local copies, waits for them, and re-layouts: 10.9 us -> 11.9 us
  transfers between devices with their start and end apart: 13 -> 13, of which waited for: 4 -> 3; matrix products, arithmetic and copies ran while one was open for 25% -> 33% of each run, Pallas kernels for 0% -> 0%
where the time goes in v1:
time: 73.6 us; the launch traced here: 73.2 us
  starting transfers between devices  22.3 us (30%)
  waiting for transfers between devices  16.6 us (23%)
  local copies, waits for them, and re-layouts  14 us (19%)
  matrix products  12.9 us (18%)
  other arithmetic  7.08 us (10%)
    ppermute x3, waiting for transfers between devices, spread(): lax.ppermute(piece, 'groups', [(a, (a + s) % ng) for a in range(ng)])  16.6 us
    unnamed x27, local copies, waits for them, and re-layouts  11.9 us
    ppermute x3, starting transfers between devices, _exclusive_prefix(): lax.ppermute(x, 'frames', [(i, i + d) for i in range(nf - d)])  8.99 us
    dot_general x1, matrix products, _project(): projected = jnp.dot(matched, weights, preferred_element_type=jnp.float32)  8.07 us
    ppermute x2, starting transfers between devices, _ring_out_proj(): piece_a = lax.ppermute(piece_a, 'frames', forward)  3.9 us
    ppermute x3, starting transfers between devices, spread(): lax.ppermute(piece, 'groups', [(a, (a + s) % ng) for a in range(ng)])  3.68 us
    all_to_all x1, starting transfers between devices, _project(): lax.all_to_all(attended, 'heads', split_axis=0, concat_axis=1, tiled=True)  3.51 us
    dot_general x1, matrix products, _attend(): jnp.einsum('fti,ftj->fij', key_pos, value_frames, preferred_element_type=...  2.65 us
  transfers between devices with their start and end apart: 13, of which 3 were waited for; matrix products, arithmetic and copies ran while one was open for 33% of the time, Pallas kernels for 0%

profile of v1, /device:TPU:0, one launch (start us, length us, event | category | flops | bytes accessed | tf_op | source)
XLA Modules:
  0.0 73.2 jit_solution(4078557654066344320)
XLA Ops:
  0.0 1.7 %constant_dynamic-update-slice_fusion.6 = (bf16[896,2240]{1,0:T(8,128)(2,1)}, bf16[56,2240]{1,0:T(8,128)(2,1)}) fusion(bf16[224,2240]{1,0:T(8,128)(2,1)} %param.11, s32[]{:T(128)S(6)} %select_n.76), kind=kLoop, calls=%fused_computation.59 | loop fusion | bytes 766980
  1.8 3.1 %collective-permute-start.3 = (bf16[56,2240]{1,0:T(8,128)(2,1)}, bf16[56,2240]{1,0:T(8,128)(2,1)S(1)}, u32[]{:S(2)}, u32[]{:S(2)}) collective-permute-start(bf16[56,2240]{1,0:T(8,128)(2,1)} %get-tuple-element.6), channel_id=1, source_target_pairs={{0,4},{4,8},{8,12},{12,0},{1,5},{5,9},{9,13},{13,1},{2,6},{6,10},{... | collective-permute-start | bytes 752648 | tf_op jit(solution)/shard_map/ppermute | solution.py:53
  4.8 2.0 %collective-permute-start.6 = (bf16[56,2240]{1,0:T(8,128)(2,1)}, bf16[56,2240]{1,0:T(8,128)(2,1)S(1)}, u32[]{:S(2)}, u32[]{:S(2)}) collective-permute-start(bf16[56,2240]{1,0:T(8,128)(2,1)} %get-tuple-element.6), channel_id=1, source_target_pairs={{0,12},{4,0},{8,4},{12,8},{1,13},{5,1},{9,5},{13,9},{2,14},{6,2},{... | collective-permute-start | bytes 752648 | tf_op jit(solution)/shard_map/ppermute | solution.py:55
  6.9 1.2 %broadcast_maximum_fusion = bf16[2048,224]{0,1:T(8,128)(2,1)S(1)} fusion(bf16[2048,224]{0,1:T(8,128)(2,1)} %param.8), kind=kLoop, calls=%fused_computation.26 | loop fusion | flops 458752 | bytes 1835008 | tf_op jit(solution)/shard_map/max | solution.py:79
  8.1 1.4 %convert_reduce_fusion.1 = f32[224]{0:T(256)S(1)} fusion(bf16[2048,224]{0,1:T(8,128)(2,1)} %param.8), kind=kLoop, calls=%fused_computation.7 | loop fusion | flops 1376032 | bytes 918400 | tf_op jit(solution)/shard_map/reduce_sum | solution.py:90
  9.7 2.7 %fusion.28 = (f32[224,224]{1,0:T(8,128)S(1)}, f32[4,224,224]{2,1,0:T(8,128)}) fusion(bf16[28,4,8,512]{3,2,1,0:T(8,128)(2,1)} %bitcast.77, bf16[28,4,8,512]{3,2,1,0:T(8,128)(2,1)S(1)} %bitcast.67, pred[224,224]{1,0:T(8,128)(4,1)S(1)} %broadcast_compare_fusion), kind=kOutput, calls=%fused_computation.77 | convolution fusion | flops 205872128 | bytes 2888704 | tf_op jit(solution)/shard_map/fti,ftj->fij/dot_general | solution.py:84
  13.2 2.6 %collective-permute-start = (f32[2,113,112]{2,1,0:T(8,128)}, f32[2,113,112]{2,1,0:T(8,128)}, u32[]{:S(2)}, u32[]{:S(2)}) collective-permute-start(f32[2,113,112]{2,1,0:T(8,128)} %pad_maximum_fusion.3), channel_id=1, source_target_pairs={{0,4},{4,8},{8,12},{1,5},{5,9},{9,13},{2,6},{6,10},{10,14},{3,7},{... | collective-permute-start | bytes 303752 | tf_op jit(solution)/shard_map/ppermute | solution.py:17
  15.7 4.5 %collective-permute-start.1 = (f32[2,113,112]{2,1,0:T(8,128)}, f32[2,113,112]{2,1,0:T(8,128)}, u32[]{:S(2)}, u32[]{:S(2)}) collective-permute-start(f32[2,113,112]{2,1,0:T(8,128)} %pad_maximum_fusion.3), channel_id=1, source_target_pairs={{0,8},{4,12},{1,9},{5,13},{2,10},{6,14},{3,11},{7,15},{16,24},{20,... | collective-permute-start | bytes 303752 | tf_op jit(solution)/shard_map/ppermute | solution.py:17
  20.2 1.9 %collective-permute-start.2 = (f32[2,113,112]{2,1,0:T(8,128)}, f32[2,113,112]{2,1,0:T(8,128)}, u32[]{:S(2)}, u32[]{:S(2)}) collective-permute-start(f32[2,113,112]{2,1,0:T(8,128)} %pad_maximum_fusion.3), channel_id=1, source_target_pairs={{0,12},{1,13},{2,14},{3,15},{16,28},{17,29},{18,30},{19,31}} | collective-permute-start | bytes 303752 | tf_op jit(solution)/shard_map/ppermute | solution.py:17
  23.3 1.2 %broadcast_maximum_fusion.1 = bf16[2048,224]{0,1:T(8,128)(2,1)S(1)} fusion(bf16[2048,224]{0,1:T(8,128)(2,1)} %param.7), kind=kLoop, calls=%fused_computation.27 | loop fusion | flops 458752 | bytes 1835008 | tf_op jit(solution)/shard_map/max | solution.py:78
  26.4 0.7 dynamic-slice_dynamic-update-slice_fusion
  27.4 1.0 %add_add_fusion = f32[2,113,112]{2,1,0:T(8,128)S(1)} fusion(f32[2,113,112]{2,1,0:T(8,128)} %collective-permute-done.2, f32[2,113,112]{2,1,0:T(8,128)} %collective-permute-done, f32[2,113,112]{2,1,0:T(8,128)} %collective-permute-done.1), kind=kLoop, calls=%fused_computation.48 | loop fusion | flops 50624 | bytes 404992 | tf_op jit(solution)/shard_map/add | solution.py:17
  29.7 1.6 %divide_convert_fusion = bf16[4,512,224]{1,2,0:T(8,128)(2,1)} fusion(f32[4,512,224]{1,2,0:T(8,128)S(1)} %fusion.11, bf16[28,4,8,512]{3,2,1,0:T(8,128)(2,1)S(1)} %bitcast.69, pred[224,224]{1,0:T(8,128)(4,1)S(1)} %copy-done.4, bf16[4,224]{1,0:T(4,128)(2,1)S(1)} %copy.18), kind=kOutput, calls=%fused_computation.5 | convolution fusion | flops 207097856 | bytes 3721984 | tf_op jit(solution)/shard_map/fti,fij->ftj/dot_general | solution.py:114
  31.3 3.5 %all-to-all-start = ((bf16[4,512,224]{1,2,0:T(8,128)(2,1)}), bf16[4,512,224]{1,2,0:T(8,128)(2,1)S(1)}, u32[]{:S(2)}, u32[]{:S(2)}) async-start(bf16[4,512,224]{1,2,0:T(8,128)(2,1)} %divide_convert_fusion), calls=%async_computation | async-start | bytes 1835008 | tf_op jit(solution)/shard_map/all_to_all | solution.py:130
  34.8 1.6 %collective-permute-start.4 = (bf16[56,2240]{1,0:T(8,128)(2,1)S(1)}, bf16[56,2240]{1,0:T(8,128)(2,1)S(1)}, u32[]{:S(2)}, u32[]{:S(2)}) collective-permute-start(bf16[56,2240]{1,0:T(8,128)(2,1)S(1)} %collective-permute-done.3), channel_id=1, source_target_pairs={{0,16},{16,0},{1,17},{17,1},{2,18},{18,2},{3,19},{19,3},{4,20},{20... | collective-permute-start | bytes 752648 | tf_op jit(solution)/shard_map/ppermute | solution.py:42
  36.4 0.8 %collective-permute-start.9 = (bf16[56,2240]{1,0:T(8,128)(2,1)S(1)}, bf16[56,2240]{1,0:T(8,128)(2,1)S(1)}, u32[]{:S(2)}, u32[]{:S(2)}) collective-permute-start(bf16[56,2240]{1,0:T(8,128)(2,1)S(1)} %collective-permute-done.3), channel_id=1, source_target_pairs={{0,4},{4,8},{8,12},{12,0},{1,5},{5,9},{9,13},{13,1},{2,6},{6,10},{... | collective-permute-start | bytes 752648 | tf_op jit(solution)/shard_map/ppermute | solution.py:53
  37.8 0.7 constant_dynamic-update-slice_fusion.5
  38.5 5.5 %collective-permute-done.4 = bf16[56,2240]{1,0:T(8,128)(2,1)S(1)} collective-permute-done((bf16[56,2240]{1,0:T(8,128)(2,1)S(1)}, bf16[56,2240]{1,0:T(8,128)(2,1)S(1)}, u32[]{:S(2)}, u32[]{:S(2)}) %collective-permute-start.4) | collective-permute-done | bytes 250912 | tf_op jit(solution)/shard_map/ppermute | solution.py:42
  44.1 4.8 %collective-permute-done.7 = bf16[56,2240]{1,0:T(8,128)(2,1)S(1)} collective-permute-done((bf16[56,2240]{1,0:T(8,128)(2,1)S(1)}, bf16[56,2240]{1,0:T(8,128)(2,1)S(1)}, u32[]{:S(2)}, u32[]{:S(2)}) %collective-permute-start.7) | collective-permute-done | bytes 250912 | tf_op jit(solution)/shard_map/ppermute | solution.py:42
  49.1 1.6 %collective-permute-start.10 = (bf16[56,2240]{1,0:T(8,128)(2,1)S(1)}, bf16[56,2240]{1,0:T(8,128)(2,1)S(1)}, u32[]{:S(2)}, u32[]{:S(2)}) collective-permute-start(bf16[56,2240]{1,0:T(8,128)(2,1)S(1)} %collective-permute-done.9), channel_id=1, source_target_pairs={{0,16},{16,0},{1,17},{17,1},{2,18},{18,2},{3,19},{19,3},{4,20},{20... | collective-permute-start | bytes 752648 | tf_op jit(solution)/shard_map/ppermute | solution.py:42
  50.7 0.7 constant_dynamic-update-slice_fusion.4
  51.4 6.3 %collective-permute-done.10 = bf16[56,2240]{1,0:T(8,128)(2,1)S(1)} collective-permute-done((bf16[56,2240]{1,0:T(8,128)(2,1)S(1)}, bf16[56,2240]{1,0:T(8,128)(2,1)S(1)}, u32[]{:S(2)}, u32[]{:S(2)}) %collective-permute-start.10) | collective-permute-done | bytes 250912 | tf_op jit(solution)/shard_map/ppermute | solution.py:42
  57.9 0.7 fusion.22
  58.6 0.7 fusion.21
  59.3 0.8 %constant_dynamic-update-slice_fusion.3 = bf16[896,2240]{1,0:T(8,128)(2,1)} fusion(bf16[896,2240]{1,0:T(8,128)(2,1)} %fusion.21, bf16[56,2240]{1,0:T(8,128)(2,1)S(1)} %collective-permute-done.6), kind=kLoop, calls=%fused_computation.56 | loop fusion | bytes 508928
  60.0 0.7 constant_dynamic-update-slice_fusion.2
  60.8 0.7 fusion.20
  61.5 0.7 %fusion.19 = bf16[896,2240]{1,0:T(8,128)(2,1)} fusion(bf16[896,2240]{1,0:T(8,128)(2,1)} %fusion.20, bf16[2,56,2240]{2,1,0:T(8,128)(2,1)S(1)} %collective-permute-done.8), kind=kLoop, calls=%fused_computation.34 | loop fusion | bytes 508928
  62.2 0.7 %constant_dynamic-update-slice_fusion.1 = bf16[896,2240]{1,0:T(8,128)(2,1)} fusion(bf16[896,2240]{1,0:T(8,128)(2,1)} %fusion.19, bf16[56,2240]{1,0:T(8,128)(2,1)S(1)} %collective-permute-done.9), kind=kLoop, calls=%fused_computation.54 | loop fusion | bytes 508928
  63.0 0.7 constant_dynamic-update-slice_fusion
  64.4 0.7 fusion.17
  65.1 8.1 %fusion.1 = bf16[512,2240]{0,1:T(8,128)(2,1)} fusion(bf16[896,2240]{1,0:T(8,128)(2,1)} %fusion.17, bf16[512,2240]{0,1:T(8,128)(2,1)} %param.10, f32[2240]{0:T(1024)S(1)} %dynamic-slice_reduce_fusion, bf16[512,896]{0,1:T(8,128)(2,1)S(1)} %bitcast.76, s32[896]{0:T(1024)S(1)} %add.167), kind=kOutput, calls=%fused_computation.2 | convolution fusion | flops 2883141632 | bytes 9531648 | tf_op jit(solution)/shard_map/dot_general | solution.py:140
  (56 shorter events, 6.9 us)
Async XLA Ops:
  0.0 27.1 %copy-start = (f32[4,2240]{1,0:T(4,128)S(1)}, f32[4,2240]{1,0:T(4,128)}, u32[]{:S(2)}) copy-start(f32[4,2240]{1,0:T(4,128)} %param.12) | copy-start | bytes 107524
  1.8 33.1 %collective-permute-start.3 = (bf16[56,2240]{1,0:T(8,128)(2,1)}, bf16[56,2240]{1,0:T(8,128)(2,1)S(1)}, u32[]{:S(2)}, u32[]{:S(2)}) collective-permute-start(bf16[56,2240]{1,0:T(8,128)(2,1)} %get-tuple-element.6), channel_id=1, source_target_pairs={{0,4},{4,8},{8,12},{12,0},{1,5},{5,9},{9,13},{13,1},{2,6},{6,10},{... | collective-permute-start | bytes 752648 | tf_op jit(solution)/shard_map/ppermute | solution.py:53
  4.8 32.5 %collective-permute-start.6 = (bf16[56,2240]{1,0:T(8,128)(2,1)}, bf16[56,2240]{1,0:T(8,128)(2,1)S(1)}, u32[]{:S(2)}, u32[]{:S(2)}) collective-permute-start(bf16[56,2240]{1,0:T(8,128)(2,1)} %get-tuple-element.6), channel_id=1, source_target_pairs={{0,12},{4,0},{8,4},{12,8},{1,13},{5,1},{9,5},{13,9},{2,14},{6,2},{... | collective-permute-start | bytes 752648 | tf_op jit(solution)/shard_map/ppermute | solution.py:55
  6.8 16.0 %copy-start.5 = (s32[4]{0:T(128)S(1)}, s32[4]{0:T(128)}, u32[]{:S(2)}) copy-start(s32[4]{0:T(128)} %constant.99.clone) | copy-start | bytes 52
  9.7 2.7 %copy-start.3 = (pred[224,224]{1,0:T(8,128)(4,1)}, pred[224,224]{1,0:T(8,128)(4,1)S(1)}, u32[]{:S(2)}) copy-start(pred[224,224]{1,0:T(8,128)(4,1)S(1)} %broadcast_compare_fusion) | copy-start | bytes 150532
  9.7 15.3 %copy-start.1 = (bf16[224,2240]{1,0:T(8,128)(2,1)S(1)}, bf16[224,2240]{1,0:T(8,128)(2,1)}, u32[]{:S(2)}) copy-start(bf16[224,2240]{1,0:T(8,128)(2,1)} %param.11) | copy-start | bytes 3010564
  13.2 14.2 %collective-permute-start = (f32[2,113,112]{2,1,0:T(8,128)}, f32[2,113,112]{2,1,0:T(8,128)}, u32[]{:S(2)}, u32[]{:S(2)}) collective-permute-start(f32[2,113,112]{2,1,0:T(8,128)} %pad_maximum_fusion.3), channel_id=1, source_target_pairs={{0,4},{4,8},{8,12},{1,5},{5,9},{9,13},{2,6},{6,10},{10,14},{3,7},{... | collective-permute-start | bytes 303752 | tf_op jit(solution)/shard_map/ppermute | solution.py:17
  15.7 11.7 %collective-permute-start.1 = (f32[2,113,112]{2,1,0:T(8,128)}, f32[2,113,112]{2,1,0:T(8,128)}, u32[]{:S(2)}, u32[]{:S(2)}) collective-permute-start(f32[2,113,112]{2,1,0:T(8,128)} %pad_maximum_fusion.3), channel_id=1, source_target_pairs={{0,8},{4,12},{1,9},{5,13},{2,10},{6,14},{3,11},{7,15},{16,24},{20,... | collective-permute-start | bytes 303752 | tf_op jit(solution)/shard_map/ppermute | solution.py:17
  20.2 7.2 %collective-permute-start.2 = (f32[2,113,112]{2,1,0:T(8,128)}, f32[2,113,112]{2,1,0:T(8,128)}, u32[]{:S(2)}, u32[]{:S(2)}) collective-permute-start(f32[2,113,112]{2,1,0:T(8,128)} %pad_maximum_fusion.3), channel_id=1, source_target_pairs={{0,12},{1,13},{2,14},{3,15},{16,28},{17,29},{18,30},{19,31}} | collective-permute-start | bytes 303752 | tf_op jit(solution)/shard_map/ppermute | solution.py:17
  24.9 4.1 %copy-start.2 = (f32[4,224,224]{2,1,0:T(8,128)S(1)}, f32[4,224,224]{2,1,0:T(8,128)}, u32[]{:S(2)}) copy-start(f32[4,224,224]{2,1,0:T(8,128)} %get-tuple-element.10) | copy-start | bytes 2408452
  27.1 2.6 %copy-start.4 = (pred[224,224]{1,0:T(8,128)(4,1)S(1)}, pred[224,224]{1,0:T(8,128)(4,1)}, u32[]{:S(2)}) copy-start(pred[224,224]{1,0:T(8,128)(4,1)} %copy-done.3) | copy-start | bytes 150532
  31.3 33.8 %all-to-all-start = ((bf16[4,512,224]{1,2,0:T(8,128)(2,1)}), bf16[4,512,224]{1,2,0:T(8,128)(2,1)S(1)}, u32[]{:S(2)}, u32[]{:S(2)}) async-start(bf16[4,512,224]{1,2,0:T(8,128)(2,1)} %divide_convert_fusion), calls=%async_computation | async-start | bytes 1835008 | tf_op jit(solution)/shard_map/all_to_all | solution.py:130
  34.8 9.2 %collective-permute-start.4 = (bf16[56,2240]{1,0:T(8,128)(2,1)S(1)}, bf16[56,2240]{1,0:T(8,128)(2,1)S(1)}, u32[]{:S(2)}, u32[]{:S(2)}) collective-permute-start(bf16[56,2240]{1,0:T(8,128)(2,1)S(1)} %collective-permute-done.3), channel_id=1, source_target_pairs={{0,16},{16,0},{1,17},{17,1},{2,18},{18,2},{3,19},{19,3},{4,20},{20... | collective-permute-start | bytes 752648 | tf_op jit(solution)/shard_map/ppermute | solution.py:42
  36.4 12.7 %collective-permute-start.9 = (bf16[56,2240]{1,0:T(8,128)(2,1)S(1)}, bf16[56,2240]{1,0:T(8,128)(2,1)S(1)}, u32[]{:S(2)}, u32[]{:S(2)}) collective-permute-start(bf16[56,2240]{1,0:T(8,128)(2,1)S(1)} %collective-permute-done.3), channel_id=1, source_target_pairs={{0,4},{4,8},{8,12},{12,0},{1,5},{5,9},{9,13},{13,1},{2,6},{6,10},{... | collective-permute-start | bytes 752648 | tf_op jit(solution)/shard_map/ppermute | solution.py:53
  37.3 11.7 %collective-permute-start.7 = (bf16[56,2240]{1,0:T(8,128)(2,1)S(1)}, bf16[56,2240]{1,0:T(8,128)(2,1)S(1)}, u32[]{:S(2)}, u32[]{:S(2)}) collective-permute-start(bf16[56,2240]{1,0:T(8,128)(2,1)S(1)} %collective-permute-done.6), channel_id=1, source_target_pairs={{0,16},{16,0},{1,17},{17,1},{2,18},{18,2},{3,19},{19,3},{4,20},{20... | collective-permute-start | bytes 752648 | tf_op jit(solution)/shard_map/ppermute | solution.py:42
  44.0 13.8 %collective-permute-start.5 = (bf16[2,56,2240]{2,1,0:T(8,128)(2,1)S(1)}, bf16[2,56,2240]{2,1,0:T(8,128)(2,1)S(1)}, u32[]{:S(2)}, u32[]{:S(2)}) collective-permute-start(bf16[2,56,2240]{2,1,0:T(8,128)(2,1)S(1)} %pad_maximum_fusion), channel_id=1, source_target_pairs={{0,1},{1,0},{2,3},{3,2},{4,5},{5,4},{6,7},{7,6},{8,9},{9,8},{10,11... | collective-permute-start | bytes 1505288 | tf_op jit(solution)/shard_map/ppermute | solution.py:45
  49.0 11.8 %collective-permute-start.8 = (bf16[2,56,2240]{2,1,0:T(8,128)(2,1)S(1)}, bf16[2,56,2240]{2,1,0:T(8,128)(2,1)S(1)}, u32[]{:S(2)}, u32[]{:S(2)}) collective-permute-start(bf16[2,56,2240]{2,1,0:T(8,128)(2,1)S(1)} %pad_maximum_fusion.1), channel_id=1, source_target_pairs={{0,1},{1,0},{2,3},{3,2},{4,5},{5,4},{6,7},{7,6},{8,9},{9,8},{10,11... | collective-permute-start | bytes 1505288 | tf_op jit(solution)/shard_map/ppermute | solution.py:45
  49.1 8.6 %collective-permute-start.10 = (bf16[56,2240]{1,0:T(8,128)(2,1)S(1)}, bf16[56,2240]{1,0:T(8,128)(2,1)S(1)}, u32[]{:S(2)}, u32[]{:S(2)}) collective-permute-start(bf16[56,2240]{1,0:T(8,128)(2,1)S(1)} %collective-permute-done.9), channel_id=1, source_target_pairs={{0,16},{16,0},{1,17},{17,1},{2,18},{18,2},{3,19},{19,3},{4,20},{20... | collective-permute-start | bytes 752648 | tf_op jit(solution)/shard_map/ppermute | solution.py:42
  57.8 5.9 %collective-permute-start.11 = (bf16[2,56,2240]{2,1,0:T(8,128)(2,1)S(1)}, bf16[2,56,2240]{2,1,0:T(8,128)(2,1)S(1)}, u32[]{:S(2)}, u32[]{:S(2)}) collective-permute-start(bf16[2,56,2240]{2,1,0:T(8,128)(2,1)S(1)} %pad_maximum_fusion.2), channel_id=1, source_target_pairs={{0,1},{1,0},{2,3},{3,2},{4,5},{5,4},{6,7},{7,6},{8,9},{9,8},{10,11... | collective-permute-start | bytes 1505288 | tf_op jit(solution)/shard_map/ppermute | solution.py:45

commit v2 on v0

--- a/solution.py
+++ b/solution.py
@@ -11,17 +11,13 @@
 
 
 def _exclusive_prefix(x, nf):
-    if nf <= 8:
-        total = jnp.zeros_like(x)
-        for d in range(1, nf):
-            total = total + lax.ppermute(x, "frames", [(i, i + d) for i in range(nf - d)])
-        return total
-    y = lax.ppermute(x, "frames", [(i, i + 1) for i in range(nf - 1)])
-    covered = 1
-    while covered < nf - 1:
-        y = y + lax.ppermute(y, "frames", [(i, i + covered) for i in range(nf - covered)])
-        covered *= 2
-    return y
+    i = lax.axis_index("frames")
+    later = jnp.arange(nf, dtype=jnp.int32) > i
+    outgoing = jnp.where(
+        later.reshape((nf,) + (1,) * x.ndim), jnp.broadcast_to(x, (nf,) + x.shape), 0.0
+    )
+    incoming = lax.all_to_all(outgoing, "frames", split_axis=0, concat_axis=0, tiled=True)
+    return jnp.sum(incoming, axis=0)
 
 
 def _ring_out_proj(out_proj, nf, nh, ng):

time: 75.8 us -> 67.2 us (0.89)
  waiting for transfers between devices: 22.6 us -> 13 us
  starting transfers between devices: 19.6 us -> 16.7 us
  local copies, waits for them, and re-layouts: 13 us -> 15.4 us
  other arithmetic: 7.16 us -> 8.46 us
    ppermute x3 -> x0, starting transfers between devices: 12 us -> none  [_exclusive_prefix(): lax.ppermute(x, 'frames', [(i, i + d) for i in range(nf - d)])]
    ppermute x3, waiting for transfers between devices: 11.6 us -> 2.87 us  [_ring_out_proj(): piece = lax.ppermute(piece, 'frames', ring)]
    ppermute x3, starting transfers between devices: 0.23 us -> 5.34 us  [_ring_out_proj(): piece = lax.ppermute(piece, 'frames', ring)]
    all_to_all x0 -> x1, starting transfers between devices: none -> 3.86 us  [_exclusive_prefix(): lax.all_to_all(outgoing, 'frames', split_axis=0, concat_axis=0, tiled=True)]
    unnamed x25 -> x19, local copies, waits for them, and re-layouts: 10.9 us -> 13 us
    another operation x1, other arithmetic: 0.09 us -> 1.29 us  [_attend(): prefix_state = earlier_state[None] + jnp.cumsum(frame_state, axis=0)]
    add x1 -> x0, other arithmetic: 1.04 us -> none  [_exclusive_prefix(): total + lax.ppermute(x, 'frames', [(i, i + d) for i in range(nf - d)])]
    another operation x3, other arithmetic: 0.15 us -> 1.09 us  [_ring_out_proj(): from_core = lax.ppermute(jnp.stack(from_groups), 'heads', swap)]
  transfers between devices with their start and end apart: 13 -> 11, of which waited for: 4 -> 3; matrix products, arithmetic and copies ran while one was open for 25% -> 40% of each run, Pallas kernels for 0% -> 0%
where the time goes in v2:
time: 67.2 us; the launch traced here: 66.5 us
  starting transfers between devices  16.7 us (25%)
  local copies, waits for them, and re-layouts  15.4 us (23%)
  waiting for transfers between devices  13 us (19%)
  matrix products  12.8 us (19%)
  other arithmetic  8.46 us (13%)
    unnamed x19, local copies, waits for them, and re-layouts  13 us
    ppermute x3, waiting for transfers between devices, _ring_out_proj(): lax.ppermute(piece, 'groups', [(a, (a + s) % ng) for a in range(ng)])  10.1 us
    dot_general x1, matrix products, _project(): projected = jnp.dot(matched, weights, preferred_element_type=jnp.float32)  8.07 us
    ppermute x3, starting transfers between devices, _ring_out_proj(): piece = lax.ppermute(piece, 'frames', ring)  5.34 us
    all_to_all x1, starting transfers between devices, _exclusive_prefix(): lax.all_to_all(outgoing, 'frames', split_axis=0, concat_axis=0, tiled=True)  3.86 us
    ppermute x3, starting transfers between devices, _ring_out_proj(): lax.ppermute(piece, 'groups', [(a, (a + s) % ng) for a in range(ng)])  3.63 us
    all_to_all x1, starting transfers between devices, _project(): lax.all_to_all(attended, 'heads', split_axis=0, concat_axis=1, tiled=True)  3.51 us
    ppermute x3, waiting for transfers between devices, _ring_out_proj(): piece = lax.ppermute(piece, 'frames', ring)  2.87 us
  transfers between devices with their start and end apart: 11, of which 3 were waited for; matrix products, arithmetic and copies ran while one was open for 40% of the time, Pallas kernels for 0%

profile of v2, /device:TPU:0, one launch (start us, length us, event | category | flops | bytes accessed | tf_op | source)
XLA Modules:
  0.0 66.5 jit_solution(845241443478756863)
XLA Ops:
  0.0 1.8 %constant_dynamic-update-slice_fusion.6 = (bf16[896,2240]{1,0:T(8,128)(2,1)}, bf16[56,2240]{1,0:T(8,128)(2,1)}) fusion(bf16[224,2240]{1,0:T(8,128)(2,1)} %param.10, s32[]{:T(128)S(6)} %select_n.85), kind=kLoop, calls=%fused_computation.60 | loop fusion | bytes 766980
  1.8 3.1 %collective-permute-start = (bf16[56,2240]{1,0:T(8,128)(2,1)}, bf16[56,2240]{1,0:T(8,128)(2,1)}, u32[]{:S(2)}, u32[]{:S(2)}) collective-permute-start(bf16[56,2240]{1,0:T(8,128)(2,1)} %get-tuple-element.6), channel_id=1, source_target_pairs={{0,4},{4,8},{8,12},{12,0},{1,5},{5,9},{9,13},{13,1},{2,6},{6,10},{... | collective-permute-start | bytes 752648 | tf_op jit(solution)/shard_map/ppermute | solution.py:35
  4.9 1.2 %broadcast_maximum_fusion = bf16[2048,224]{0,1:T(8,128)(2,1)S(1)} fusion(bf16[2048,224]{0,1:T(8,128)(2,1)} %param.7), kind=kLoop, calls=%fused_computation.26 | loop fusion | flops 458752 | bytes 1835008 | tf_op jit(solution)/shard_map/max | solution.py:60
  6.1 1.4 %convert_reduce_fusion.1 = f32[224]{0:T(256)S(1)} fusion(bf16[2048,224]{0,1:T(8,128)(2,1)} %param.7), kind=kLoop, calls=%fused_computation.7 | loop fusion | flops 1376032 | bytes 918400 | tf_op jit(solution)/shard_map/reduce_sum | solution.py:71
  7.6 2.6 %fusion.28 = (f32[224,224]{1,0:T(8,128)S(1)}, f32[4,224,224]{2,1,0:T(8,128)}) fusion(bf16[28,4,8,512]{3,2,1,0:T(8,128)(2,1)} %bitcast.80, bf16[28,4,8,512]{3,2,1,0:T(8,128)(2,1)S(1)} %bitcast.69, pred[224,224]{1,0:T(8,128)(4,1)S(1)} %broadcast_compare_fusion), kind=kOutput, calls=%fused_computation.78 | convolution fusion | flops 205872128 | bytes 2888704 | tf_op jit(solution)/shard_map/fti,ftj->fij/dot_general | solution.py:65
  10.5 0.9 %broadcast_select_fusion = f32[4,2,113,112]{2,3,1,0:T(8,128)} fusion(f32[2,113,112]{1,2,0:T(8,128)S(1)} %copy.41, pred[4]{0:T(512)(128)(4,1)S(1)} %iota_compare_fusion.6), kind=kLoop, calls=%fused_computation.47 | loop fusion | flops 101248 | bytes 506244 | tf_op jit(solution)/shard_map/jit(_where)/select_n | solution.py:16
  11.4 3.9 %all-to-all-start = ((f32[4,2,113,112]{2,3,1,0:T(8,128)}), f32[4,2,113,112]{2,3,1,0:T(8,128)S(1)}, u32[]{:S(2)}, u32[]{:S(2)}) async-start(f32[4,2,113,112]{2,3,1,0:T(8,128)} %broadcast_select_fusion), calls=%async_computation | async-start | bytes 917504 | tf_op jit(solution)/shard_map/all_to_all | solution.py:19
  16.4 1.2 %broadcast_maximum_fusion.1 = bf16[2048,224]{0,1:T(8,128)(2,1)S(1)} fusion(bf16[2048,224]{0,1:T(8,128)(2,1)} %param.6), kind=kLoop, calls=%fused_computation.27 | loop fusion | flops 458752 | bytes 1835008 | tf_op jit(solution)/shard_map/max | solution.py:59
  18.1 0.7 %dynamic-slice_dynamic-update-slice_fusion.2 = bf16[896,2240]{1,0:T(8,128)(2,1)} fusion(bf16[896,2240]{1,0:T(8,128)(2,1)} %get-tuple-element.5, bf16[224,2240]{1,0:T(8,128)(2,1)S(1)} %copy-done.1, s32[]{:T(128)S(6)} %select_n.86), kind=kLoop, calls=%fused_computation.43 | loop fusion | bytes 508932
  18.8 0.7 %dynamic-slice_dynamic-update-slice_fusion.1 = bf16[896,2240]{1,0:T(8,128)(2,1)} fusion(bf16[896,2240]{1,0:T(8,128)(2,1)} %dynamic-slice_dynamic-update-slice_fusion.2, bf16[224,2240]{1,0:T(8,128)(2,1)S(1)} %copy-done.1, s32[]{:T(128)S(6)} %select_n.87), kind=kLoop, calls=%fused_computation.42 | loop fusion | bytes 508932
  19.8 0.7 %dynamic-slice_dynamic-update-slice_fusion = bf16[896,2240]{1,0:T(8,128)(2,1)} fusion(bf16[896,2240]{1,0:T(8,128)(2,1)} %dynamic-slice_dynamic-update-slice_fusion.1, bf16[224,2240]{1,0:T(8,128)(2,1)S(1)} %copy-done.1, s32[]{:T(128)S(6)} %select_n.88), kind=kLoop, calls=%fused_computation.41 | loop fusion | bytes 508932
  20.5 1.5 %collective-permute-start.1 = (bf16[56,2240]{1,0:T(8,128)(2,1)}, bf16[56,2240]{1,0:T(8,128)(2,1)S(1)}, u32[]{:S(2)}, u32[]{:S(2)}) collective-permute-start(bf16[56,2240]{1,0:T(8,128)(2,1)} %collective-permute-done), channel_id=1, source_target_pairs={{0,16},{16,0},{1,17},{17,1},{2,18},{18,2},{3,19},{19,3},{4,20},{20... | collective-permute-start | bytes 752648 | tf_op jit(solution)/shard_map/ppermute | solution.py:37
  22.0 2.0 %collective-permute-start.3 = (bf16[56,2240]{1,0:T(8,128)(2,1)}, bf16[56,2240]{1,0:T(8,128)(2,1)S(1)}, u32[]{:S(2)}, u32[]{:S(2)}) collective-permute-start(bf16[56,2240]{1,0:T(8,128)(2,1)} %collective-permute-done), channel_id=1, source_target_pairs={{0,4},{4,8},{8,12},{12,0},{1,5},{5,9},{9,13},{13,1},{2,6},{6,10},{... | collective-permute-start | bytes 752648 | tf_op jit(solution)/shard_map/ppermute | solution.py:35
  24.1 1.7 %constant_dynamic-update-slice_fusion.5 = bf16[896,2240]{1,0:T(8,128)(2,1)} fusion(bf16[896,2240]{1,0:T(8,128)(2,1)} %dynamic-slice_dynamic-update-slice_fusion, bf16[56,2240]{1,0:T(8,128)(2,1)} %collective-permute-done), kind=kLoop, calls=%fused_computation.59 | loop fusion | bytes 516096
  25.8 2.3 %collective-permute-done.1 = bf16[56,2240]{1,0:T(8,128)(2,1)S(1)} collective-permute-done((bf16[56,2240]{1,0:T(8,128)(2,1)}, bf16[56,2240]{1,0:T(8,128)(2,1)S(1)}, u32[]{:S(2)}, u32[]{:S(2)}) %collective-permute-start.1) | collective-permute-done | bytes 250912 | tf_op jit(solution)/shard_map/ppermute | solution.py:37
  28.1 1.0 %pad_maximum_fusion = bf16[2,56,2240]{2,1,0:T(8,128)(2,1)S(1)} fusion(bf16[1,56,2240]{2,1,0:T(8,128)(2,1)S(1)} %bitcast.77, bf16[1,56,2240]{2,1,0:T(8,128)(2,1)} %bitcast.10), kind=kLoop, calls=%fused_computation.22 | loop fusion | flops 250880 | bytes 1003520 | tf_op jit(solution)/shard_map/stack | solution.py:40
  29.2 2.9 %collective-permute-done.3 = bf16[56,2240]{1,0:T(8,128)(2,1)S(1)} collective-permute-done((bf16[56,2240]{1,0:T(8,128)(2,1)}, bf16[56,2240]{1,0:T(8,128)(2,1)S(1)}, u32[]{:S(2)}, u32[]{:S(2)}) %collective-permute-start.3) | collective-permute-done | bytes 250912 | tf_op jit(solution)/shard_map/ppermute | solution.py:35
  32.1 1.5 %collective-permute-start.4 = (bf16[56,2240]{1,0:T(8,128)(2,1)S(1)}, bf16[56,2240]{1,0:T(8,128)(2,1)S(1)}, u32[]{:S(2)}, u32[]{:S(2)}) collective-permute-start(bf16[56,2240]{1,0:T(8,128)(2,1)S(1)} %collective-permute-done.3), channel_id=1, source_target_pairs={{0,16},{16,0},{1,17},{17,1},{2,18},{18,2},{3,19},{19,3},{4,20},{20... | collective-permute-start | bytes 752648 | tf_op jit(solution)/shard_map/ppermute | solution.py:37
  33.8 0.7 %constant_dynamic-update-slice_fusion.4 = bf16[896,2240]{1,0:T(8,128)(2,1)} fusion(bf16[896,2240]{1,0:T(8,128)(2,1)} %constant_dynamic-update-slice_fusion.5, bf16[56,2240]{1,0:T(8,128)(2,1)S(1)} %collective-permute-done.1), kind=kLoop, calls=%fused_computation.58 | loop fusion | bytes 508928
  35.5 1.3 %fusion.5 = bf16[4,224,224]{2,1,0:T(8,128)(2,1)S(1)} fusion(f32[4,224,224]{2,1,0:T(8,128)} %get-tuple-element.10, f32[224,224]{1,0:T(8,128)S(1)} %add.133), kind=kOutput, calls=%fused_computation.12 | output fusion | flops 1003520 | bytes 1404928 | tf_op jit(solution)/shard_map/jit(cumsum)/reduce_window_sum | solution.py:86
  37.3 1.6 %divide_convert_fusion = bf16[4,512,224]{1,2,0:T(8,128)(2,1)} fusion(f32[4,512,224]{1,2,0:T(8,128)S(1)} %fusion.11, bf16[28,4,8,512]{3,2,1,0:T(8,128)(2,1)S(1)} %bitcast.71, pred[224,224]{1,0:T(8,128)(4,1)S(1)} %broadcast_compare_fusion, bf16[4,224]{1,0:T(4,128)(2,1)S(1)} %copy.45), kind=kOutput, calls=%fused_computation.5 | convolution fusion | flops 207097856 | bytes 3721984 | tf_op jit(solution)/shard_map/fti,fij->ftj/dot_general | solution.py:95
  38.9 3.5 %all-to-all-start.1 = ((bf16[4,512,224]{1,2,0:T(8,128)(2,1)}), bf16[4,512,224]{1,2,0:T(8,128)(2,1)S(1)}, u32[]{:S(2)}, u32[]{:S(2)}) async-start(bf16[4,512,224]{1,2,0:T(8,128)(2,1)} %divide_convert_fusion), calls=%async_computation.1 | async-start | bytes 1835008 | tf_op jit(solution)/shard_map/all_to_all | solution.py:111
  43.3 7.8 %collective-permute-done.7 = bf16[56,2240]{1,0:T(8,128)(2,1)S(1)} collective-permute-done((bf16[56,2240]{1,0:T(8,128)(2,1)S(1)}, bf16[56,2240]{1,0:T(8,128)(2,1)S(1)}, u32[]{:S(2)}, u32[]{:S(2)}) %collective-permute-start.7) | collective-permute-done | bytes 250912 | tf_op jit(solution)/shard_map/ppermute | solution.py:37
  51.2 0.7 %fusion.22 = bf16[896,2240]{1,0:T(8,128)(2,1)} fusion(bf16[896,2240]{1,0:T(8,128)(2,1)} %constant_dynamic-update-slice_fusion.4, bf16[2,56,2240]{2,1,0:T(8,128)(2,1)S(1)} %collective-permute-done.2), kind=kLoop, calls=%fused_computation.40 | loop fusion | bytes 508928
  51.9 0.7 %fusion.21 = bf16[896,2240]{1,0:T(8,128)(2,1)} fusion(bf16[896,2240]{1,0:T(8,128)(2,1)} %fusion.22, bf16[2,56,2240]{2,1,0:T(8,128)(2,1)S(1)} %collective-permute-done.2), kind=kLoop, calls=%fused_computation.38 | loop fusion | bytes 508928
  52.6 0.7 %constant_dynamic-update-slice_fusion.3 = bf16[896,2240]{1,0:T(8,128)(2,1)} fusion(bf16[896,2240]{1,0:T(8,128)(2,1)} %fusion.21, bf16[56,2240]{1,0:T(8,128)(2,1)S(1)} %collective-permute-done.3), kind=kLoop, calls=%fused_computation.57 | loop fusion | bytes 508928
  54.8 0.7 %fusion.19 = bf16[896,2240]{1,0:T(8,128)(2,1)} fusion(bf16[896,2240]{1,0:T(8,128)(2,1)} %fusion.20, bf16[2,56,2240]{2,1,0:T(8,128)(2,1)S(1)} %collective-permute-done.5), kind=kLoop, calls=%fused_computation.34 | loop fusion | bytes 508928
  55.5 0.7 %constant_dynamic-update-slice_fusion.1 = bf16[896,2240]{1,0:T(8,128)(2,1)} fusion(bf16[896,2240]{1,0:T(8,128)(2,1)} %fusion.19, bf16[56,2240]{1,0:T(8,128)(2,1)S(1)} %collective-permute-done.6), kind=kLoop, calls=%fused_computation.55 | loop fusion | bytes 508928
  56.3 0.7 %constant_dynamic-update-slice_fusion = bf16[896,2240]{1,0:T(8,128)(2,1)} fusion(bf16[896,2240]{1,0:T(8,128)(2,1)} %constant_dynamic-update-slice_fusion.1, bf16[56,2240]{1,0:T(8,128)(2,1)S(1)} %collective-permute-done.7), kind=kLoop, calls=%fused_computation.54 | loop fusion | bytes 508928
  57.0 0.7 %fusion.18 = bf16[896,2240]{1,0:T(8,128)(2,1)} fusion(bf16[896,2240]{1,0:T(8,128)(2,1)} %constant_dynamic-update-slice_fusion, bf16[2,56,2240]{2,1,0:T(8,128)(2,1)S(1)} %collective-permute-done.8), kind=kLoop, calls=%fused_computation.32 | loop fusion | bytes 508928
  57.7 0.7 %fusion.17 = bf16[896,2240]{1,0:T(8,128)(2,1)} fusion(bf16[896,2240]{1,0:T(8,128)(2,1)} %fusion.18, bf16[2,56,2240]{2,1,0:T(8,128)(2,1)S(1)} %collective-permute-done.8), kind=kLoop, calls=%fused_computation.30 | loop fusion | bytes 508928 | tf_op jit(solution)/shard_map/concatenate | solution.py:42
  58.5 8.1 %fusion.1 = bf16[512,2240]{0,1:T(8,128)(2,1)} fusion(bf16[896,2240]{1,0:T(8,128)(2,1)} %fusion.17, bf16[512,2240]{0,1:T(8,128)(2,1)} %param.9, f32[2240]{0:T(1024)S(1)} %dynamic-slice_reduce_fusion, bf16[512,896]{0,1:T(8,128)(2,1)S(1)} %bitcast.78, s32[896]{0:T(1024)S(1)} %add.155), kind=kOutput, calls=%fused_computation.2 | convolution fusion | flops 2883141632 | bytes 9531648 | tf_op jit(solution)/shard_map/dot_general | solution.py:121
  (48 shorter events, 6.3 us)
Async XLA Ops:
  0.0 19.5 %copy-start = (f32[4,2240]{1,0:T(4,128)S(1)}, f32[4,2240]{1,0:T(4,128)}, u32[]{:S(2)}) copy-start(f32[4,2240]{1,0:T(4,128)} %param.11) | copy-start | bytes 107524
  1.8 18.7 %collective-permute-start = (bf16[56,2240]{1,0:T(8,128)(2,1)}, bf16[56,2240]{1,0:T(8,128)(2,1)}, u32[]{:S(2)}, u32[]{:S(2)}) collective-permute-start(bf16[56,2240]{1,0:T(8,128)(2,1)} %get-tuple-element.6), channel_id=1, source_target_pairs={{0,4},{4,8},{8,12},{12,0},{1,5},{5,9},{9,13},{13,1},{2,6},{6,10},{... | collective-permute-start | bytes 752648 | tf_op jit(solution)/shard_map/ppermute | solution.py:35
  10.2 7.8 %copy-start.1 = (bf16[224,2240]{1,0:T(8,128)(2,1)S(1)}, bf16[224,2240]{1,0:T(8,128)(2,1)}, u32[]{:S(2)}) copy-start(bf16[224,2240]{1,0:T(8,128)(2,1)} %param.10) | copy-start | bytes 3010564
  11.4 23.2 %all-to-all-start = ((f32[4,2,113,112]{2,3,1,0:T(8,128)}), f32[4,2,113,112]{2,3,1,0:T(8,128)S(1)}, u32[]{:S(2)}, u32[]{:S(2)}) async-start(f32[4,2,113,112]{2,3,1,0:T(8,128)} %broadcast_select_fusion), calls=%async_computation | async-start | bytes 917504 | tf_op jit(solution)/shard_map/all_to_all | solution.py:19
  20.5 7.6 %collective-permute-start.1 = (bf16[56,2240]{1,0:T(8,128)(2,1)}, bf16[56,2240]{1,0:T(8,128)(2,1)S(1)}, u32[]{:S(2)}, u32[]{:S(2)}) collective-permute-start(bf16[56,2240]{1,0:T(8,128)(2,1)} %collective-permute-done), channel_id=1, source_target_pairs={{0,16},{16,0},{1,17},{17,1},{2,18},{18,2},{3,19},{19,3},{4,20},{20... | collective-permute-start | bytes 752648 | tf_op jit(solution)/shard_map/ppermute | solution.py:37
  22.0 10.0 %collective-permute-start.3 = (bf16[56,2240]{1,0:T(8,128)(2,1)}, bf16[56,2240]{1,0:T(8,128)(2,1)S(1)}, u32[]{:S(2)}, u32[]{:S(2)}) collective-permute-start(bf16[56,2240]{1,0:T(8,128)(2,1)} %collective-permute-done), channel_id=1, source_target_pairs={{0,4},{4,8},{8,12},{12,0},{1,5},{5,9},{9,13},{13,1},{2,6},{6,10},{... | collective-permute-start | bytes 752648 | tf_op jit(solution)/shard_map/ppermute | solution.py:35
  29.1 22.1 %collective-permute-start.2 = (bf16[2,56,2240]{2,1,0:T(8,128)(2,1)S(1)}, bf16[2,56,2240]{2,1,0:T(8,128)(2,1)S(1)}, u32[]{:S(2)}, u32[]{:S(2)}) collective-permute-start(bf16[2,56,2240]{2,1,0:T(8,128)(2,1)S(1)} %pad_maximum_fusion), channel_id=1, source_target_pairs={{0,1},{1,0},{2,3},{3,2},{4,5},{5,4},{6,7},{7,6},{8,9},{9,8},{10,11... | collective-permute-start | bytes 1505288 | tf_op jit(solution)/shard_map/ppermute | solution.py:40
  32.1 11.0 %collective-permute-start.4 = (bf16[56,2240]{1,0:T(8,128)(2,1)S(1)}, bf16[56,2240]{1,0:T(8,128)(2,1)S(1)}, u32[]{:S(2)}, u32[]{:S(2)}) collective-permute-start(bf16[56,2240]{1,0:T(8,128)(2,1)S(1)} %collective-permute-done.3), channel_id=1, source_target_pairs={{0,16},{16,0},{1,17},{17,1},{2,18},{18,2},{3,19},{19,3},{4,20},{20... | collective-permute-start | bytes 752648 | tf_op jit(solution)/shard_map/ppermute | solution.py:37
  33.6 8.9 %collective-permute-start.6 = (bf16[56,2240]{1,0:T(8,128)(2,1)S(1)}, bf16[56,2240]{1,0:T(8,128)(2,1)S(1)}, u32[]{:S(2)}, u32[]{:S(2)}) collective-permute-start(bf16[56,2240]{1,0:T(8,128)(2,1)S(1)} %collective-permute-done.3), channel_id=1, source_target_pairs={{0,4},{4,8},{8,12},{12,0},{1,5},{5,9},{9,13},{13,1},{2,6},{6,10},{... | collective-permute-start | bytes 752648 | tf_op jit(solution)/shard_map/ppermute | solution.py:35
  38.9 19.5 %all-to-all-start.1 = ((bf16[4,512,224]{1,2,0:T(8,128)(2,1)}), bf16[4,512,224]{1,2,0:T(8,128)(2,1)S(1)}, u32[]{:S(2)}, u32[]{:S(2)}) async-start(bf16[4,512,224]{1,2,0:T(8,128)(2,1)} %divide_convert_fusion), calls=%async_computation.1 | async-start | bytes 1835008 | tf_op jit(solution)/shard_map/all_to_all | solution.py:111
  42.5 8.6 %collective-permute-start.7 = (bf16[56,2240]{1,0:T(8,128)(2,1)S(1)}, bf16[56,2240]{1,0:T(8,128)(2,1)S(1)}, u32[]{:S(2)}, u32[]{:S(2)}) collective-permute-start(bf16[56,2240]{1,0:T(8,128)(2,1)S(1)} %collective-permute-done.6), channel_id=1, source_target_pairs={{0,16},{16,0},{1,17},{17,1},{2,18},{18,2},{3,19},{19,3},{4,20},{20... | collective-permute-start | bytes 752648 | tf_op jit(solution)/shard_map/ppermute | solution.py:37
  43.1 11.0 %collective-permute-start.5 = (bf16[2,56,2240]{2,1,0:T(8,128)(2,1)S(1)}, bf16[2,56,2240]{2,1,0:T(8,128)(2,1)S(1)}, u32[]{:S(2)}, u32[]{:S(2)}) collective-permute-start(bf16[2,56,2240]{2,1,0:T(8,128)(2,1)S(1)} %pad_maximum_fusion.1), channel_id=1, source_target_pairs={{0,1},{1,0},{2,3},{3,2},{4,5},{5,4},{6,7},{7,6},{8,9},{9,8},{10,11... | collective-permute-start | bytes 1505288 | tf_op jit(solution)/shard_map/ppermute | solution.py:40
  51.1 5.9 %collective-permute-start.8 = (bf16[2,56,2240]{2,1,0:T(8,128)(2,1)S(1)}, bf16[2,56,2240]{2,1,0:T(8,128)(2,1)S(1)}, u32[]{:S(2)}, u32[]{:S(2)}) collective-permute-start(bf16[2,56,2240]{2,1,0:T(8,128)(2,1)S(1)} %pad_maximum_fusion.2), channel_id=1, source_target_pairs={{0,1},{1,0},{2,3},{3,2},{4,5},{5,4},{6,7},{7,6},{8,9},{9,8},{10,11... | collective-permute-start | bytes 1505288 | tf_op jit(solution)/shard_map/ppermute | solution.py:40

commit v3 on v2

--- a/solution.py
+++ b/solution.py
@@ -28,25 +28,35 @@
     shares = [jnp.remainder(g - s, ng) * 2 + core for s in range(ng)]
     shares += [jnp.remainder(g - s, ng) * 2 + 1 - core for s in range(ng)]
     pieces = [lax.dynamic_slice_in_dim(out_proj, share * sub, sub, axis=0) for share in shares]
-    ring = [(i, (i + 1) % nf) for i in range(nf)]
+    forward = [(i, (i + 1) % nf) for i in range(nf)]
+    backward = [(i, (i - 1) % nf) for i in range(nf)]
     swap = [(a, a ^ 1) for a in range(nh)]
+    ahead = nf - 2 if nf >= 3 else nf - 1
+    offsets = [0] + [-t for t in range(1, ahead + 1)]
+    direct = None
+    if ahead < nf - 1:
+        direct = lax.ppermute(jnp.stack(pieces[:ng]), "frames", backward)
+        offsets.append(1)
     piece = pieces[0]
-    for _ in range(1, nf):
-        piece = lax.ppermute(piece, "frames", ring)
+    for _ in range(1, ahead + 1):
+        piece = lax.ppermute(piece, "frames", forward)
         from_groups = [piece] + [
             lax.ppermute(piece, "groups", [(a, (a + s) % ng) for a in range(ng)])
             for s in range(1, ng)
         ]
         from_core = lax.ppermute(jnp.stack(from_groups), "heads", swap)
         pieces += from_groups + [from_core[s] for s in range(ng)]
-    return jnp.concatenate(pieces, axis=0), jnp.stack(shares)
+    if direct is not None:
+        direct_core = lax.ppermute(direct, "heads", swap)
+        pieces += [direct[s] for s in range(ng)] + [direct_core[s] for s in range(ng)]
+    return jnp.concatenate(pieces, axis=0), jnp.stack(shares), offsets
 
 
 def make_per_device(nf, nh, ng):
     def per_device(query_heads, key_heads, value_heads, residual, out_proj, frame_gate):
-        weights, shares = _ring_out_proj(out_proj, nf, nh, ng)
+        weights, shares, offsets = _ring_out_proj(out_proj, nf, nh, ng)
         attended = _attend(query_heads, key_heads, value_heads, nf)
-        return _project(attended, weights, shares, residual, frame_gate, nf, ng)
+        return _project(attended, weights, shares, offsets, residual, frame_gate, nf, ng)
 
     return per_device
 
@@ -98,7 +108,7 @@
     return (numerator / denominator).astype(jnp.bfloat16).reshape(length, width)
 
 
-def _project(attended, weights, shares, residual, frame_gate, nf, ng):
+def _project(attended, weights, shares, offsets, residual, frame_gate, nf, ng):
     rows_here = residual.shape[0]
     head_pos = lax.axis_index("heads")
     if rows_here <= FRAME_TOK and FRAME_TOK % rows_here == 0:
@@ -113,7 +123,7 @@
     depth = weights.shape[0]
     sub = depth // (nf * nparts)
     j = lax.axis_index("frames")
-    block = jnp.remainder(j - jnp.arange(nf, dtype=jnp.int32), nf)
+    block = jnp.remainder(j + jnp.array(offsets, dtype=jnp.int32), nf)
     order = (block[:, None] * nparts + shares[None, :]).reshape(-1)
     source = (order[:, None] * sub + jnp.arange(sub, dtype=jnp.int32)[None, :]).reshape(-1)
     pick = (jnp.arange(depth, dtype=jnp.int32)[:, None] == source[None, :]).astype(jnp.bfloat16)

time: 67.2 us -> 68.9 us (1.025)
  waiting for transfers between devices: 13 us -> 6.12 us
  local copies, waits for them, and re-layouts: 15.4 us -> 22.2 us
  other arithmetic: 8.46 us -> 10.2 us
  matrix products: 12.8 us -> 11.6 us
  starting transfers between devices: 16.7 us -> 17.8 us
    ppermute x3 -> x2, waiting for transfers between devices: 10.1 us -> 2.49 us  [_ring_out_proj(): lax.ppermute(piece, 'groups', [(a, (a + s) % ng) for a in range(ng)])]
    unnamed x19 -> x26, local copies, waits for them, and re-layouts: 13 us -> 17.1 us
    another operation x2 -> x3, other arithmetic: 0.08 us -> 1.88 us  [the longest x1 1.79 us: _ring_out_proj(): direct = lax.ppermute(jnp.stack(pieces[:ng]), 'frames', backward)]
    ppermute x3 -> x4, starting transfers between devices: 5.34 us -> 7.06 us  [the longest x2 5.03 us: _ring_out_proj(): piece = lax.ppermute(piece, 'frames', forward)]
    another operation x0 -> x1, local copies, waits for them, and re-layouts: none -> 1.68 us  [_ring_out_proj(): direct = lax.ppermute(jnp.stack(pieces[:ng]), 'frames', backward)]
    reduce_sum x1, other arithmetic: 1.44 us -> 0.26 us  [_attend(): own_sum = jnp.sum(frame_sum, axis=0)]
    another operation x1, other arithmetic: 1.29 us -> 0.12 us  [_attend(): prefix_state = earlier_state[None] + jnp.cumsum(frame_state, axis=0)]
    dot_general x1, matrix products: 2.57 us -> 1.39 us  [_attend(): jnp.einsum('fti,ftj->fij', key_pos, value_frames, preferred_element_type=...]
  transfers between devices with their start and end apart: 11 -> 10, of which waited for: 3 -> 3; matrix products, arithmetic and copies ran while one was open for 40% -> 50% of each run, Pallas kernels for 0% -> 0%
where the time goes in v3:
time: 68.9 us; the launch traced here: 68.2 us
  local copies, waits for them, and re-layouts  22.2 us (32%)
  starting transfers between devices  17.8 us (26%)
  matrix products  11.6 us (17%)
  other arithmetic  10.2 us (15%)
  waiting for transfers between devices  6.12 us (9%)
    unnamed x26, local copies, waits for them, and re-layouts  17.1 us
    dot_general x1, matrix products, _project(): projected = jnp.dot(matched, weights, preferred_element_type=jnp.float32)  8.07 us
    ppermute x2, starting transfers between devices, _ring_out_proj(): piece = lax.ppermute(piece, 'frames', forward)  5.03 us
    ppermute x2, waiting for transfers between devices, _ring_out_proj(): piece = lax.ppermute(piece, 'frames', forward)  3.51 us
    all_to_all x1, starting transfers between devices, _project(): lax.all_to_all(attended, 'heads', split_axis=0, concat_axis=1, tiled=True)  3.51 us
    all_to_all x1, starting transfers between devices, _exclusive_prefix(): lax.all_to_all(outgoing, 'frames', split_axis=0, concat_axis=0, tiled=True)  3.46 us
    ppermute x2, starting transfers between devices, _ring_out_proj(): lax.ppermute(piece, 'groups', [(a, (a + s) % ng) for a in range(ng)])  3.25 us
    ppermute x2, waiting for transfers between devices, _ring_out_proj(): lax.ppermute(piece, 'groups', [(a, (a + s) % ng) for a in range(ng)])  2.49 us
  transfers between devices with their start and end apart: 10, of which 3 were waited for; matrix products, arithmetic and copies ran while one was open for 50% of the time, Pallas kernels for 0%

profile of v3, /device:TPU:0, one launch (start us, length us, event | category | flops | bytes accessed | tf_op | source)
XLA Modules:
  0.0 68.2 jit_solution(15428263222481798473)
XLA Ops:
  0.0 1.9 %constant_dynamic-update-slice_fusion.4 = (bf16[896,2240]{1,0:T(8,128)(2,1)}, bf16[56,2240]{1,0:T(8,128)(2,1)}) fusion(bf16[224,2240]{1,0:T(8,128)(2,1)} %param.11, s32[]{:T(128)S(6)} %select_n.81), kind=kLoop, calls=%fused_computation.63 | loop fusion | bytes 766980
  1.9 3.1 %collective-permute-start = (bf16[56,2240]{1,0:T(8,128)(2,1)}, bf16[56,2240]{1,0:T(8,128)(2,1)}, u32[]{:S(2)}, u32[]{:S(2)}) collective-permute-start(bf16[56,2240]{1,0:T(8,128)(2,1)} %get-tuple-element.6), channel_id=1, source_target_pairs={{0,4},{4,8},{8,12},{12,0},{1,5},{5,9},{9,13},{13,1},{2,6},{6,10},{... | collective-permute-start | bytes 752648 | tf_op jit(solution)/shard_map/ppermute | solution.py:42
  5.0 1.7 %dynamic-slice_bitcast_fusion = (bf16[1,56,2240]{2,1,0:T(8,128)(2,1)S(1)}, bf16[896,2240]{1,0:T(8,128)(2,1)}) fusion(bf16[224,2240]{1,0:T(8,128)(2,1)} %param.11, s32[]{:T(128)S(6)} %select_n.82, bf16[896,2240]{1,0:T(8,128)(2,1)} %get-tuple-element.5), kind=kLoop, calls=%fused_computation.52 | loop fusion | bytes 766980 | tf_op jit(solution)/shard_map/stack | solution.py:38
  6.7 1.8 %pad_maximum_fusion.2 = bf16[2,56,2240]{2,1,0:T(8,128)(2,1)} fusion(bf16[1,56,2240]{2,1,0:T(8,128)(2,1)S(1)} %get-tuple-element.7, bf16[1,56,2240]{2,1,0:T(8,128)(2,1)} %bitcast.18), kind=kLoop, calls=%fused_computation.24 | loop fusion | flops 250880 | bytes 1003520 | tf_op jit(solution)/shard_map/stack | solution.py:38
  8.5 2.0 %collective-permute-start.6 = (bf16[2,56,2240]{2,1,0:T(8,128)(2,1)}, bf16[2,56,2240]{2,1,0:T(8,128)(2,1)}, u32[]{:S(2)}, u32[]{:S(2)}) collective-permute-start(bf16[2,56,2240]{2,1,0:T(8,128)(2,1)} %pad_maximum_fusion.2), channel_id=1, source_target_pairs={{0,12},{4,0},{8,4},{12,8},{1,13},{5,1},{9,5},{13,9},{2,14},{6,2},{... | collective-permute-start | bytes 1505288 | tf_op jit(solution)/shard_map/ppermute | solution.py:38
  10.5 1.2 %broadcast_maximum_fusion = bf16[2048,224]{0,1:T(8,128)(2,1)S(1)} fusion(bf16[2048,224]{0,1:T(8,128)(2,1)} %param.8), kind=kLoop, calls=%fused_computation.26 | loop fusion | flops 458752 | bytes 1835008 | tf_op jit(solution)/shard_map/max | solution.py:70
  12.2 1.4 %fusion.30 = (f32[224,224]{1,0:T(8,128)S(1)}, f32[4,224,224]{2,1,0:T(8,128)}) fusion(bf16[28,4,8,512]{3,2,1,0:T(8,128)(2,1)S(1)} %bitcast.87, bf16[28,4,8,512]{3,2,1,0:T(8,128)(2,1)S(1)} %bitcast.78, pred[224,224]{1,0:T(8,128)(4,1)S(1)} %broadcast_compare_fusion), kind=kOutput, calls=%fused_computation.81 | convolution fusion | flops 205872128 | bytes 2888704 | tf_op jit(solution)/shard_map/fti,ftj->fij/dot_general | solution.py:75
  13.8 0.9 %broadcast_select_fusion = f32[4,2,113,112]{2,3,1,0:T(8,128)} fusion(f32[2,113,112]{1,2,0:T(8,128)S(1)} %copy.42, pred[4]{0:T(512)(128)(4,1)S(1)} %iota_compare_fusion.6), kind=kLoop, calls=%fused_computation.50 | loop fusion | flops 101248 | bytes 506244 | tf_op jit(solution)/shard_map/jit(_where)/select_n | solution.py:16
  14.7 3.5 %all-to-all-start = ((f32[4,2,113,112]{2,3,1,0:T(8,128)}), f32[4,2,113,112]{2,3,1,0:T(8,128)S(1)}, u32[]{:S(2)}, u32[]{:S(2)}) async-start(f32[4,2,113,112]{2,3,1,0:T(8,128)} %broadcast_select_fusion), calls=%async_computation | async-start | bytes 917504 | tf_op jit(solution)/shard_map/all_to_all | solution.py:19
  19.4 1.2 %broadcast_maximum_fusion.1 = bf16[2048,224]{0,1:T(8,128)(2,1)S(1)} fusion(bf16[2048,224]{0,1:T(8,128)(2,1)} %param.7), kind=kLoop, calls=%fused_computation.27 | loop fusion | flops 458752 | bytes 1835008 | tf_op jit(solution)/shard_map/max | solution.py:69
  20.6 1.1 %convert_reduce_fusion = f32[4,224]{0,1:T(8,128)} fusion(bf16[4,512,224]{1,0,2:T(4,128)(2,1)S(1)} %reshape.133), kind=kLoop, calls=%fused_computation.6 | loop fusion | flops 916608 | bytes 921088 | tf_op jit(solution)/shard_map/reduce_sum | solution.py:79
  21.7 0.7 %dynamic-slice_dynamic-update-slice_fusion.1 = bf16[896,2240]{1,0:T(8,128)(2,1)} fusion(bf16[896,2240]{1,0:T(8,128)(2,1)} %get-tuple-element.8, bf16[224,2240]{1,0:T(8,128)(2,1)S(1)} %copy-done.2, s32[]{:T(128)S(6)} %select_n.83), kind=kLoop, calls=%fused_computation.46 | loop fusion | bytes 508932
  22.5 1.1 %reduce_window_sum.23 = f32[4,224]{0,1:T(8,128)S(1)} reduce-window(f32[4,224]{0,1:T(8,128)} %convert_reduce_fusion, f32[]{:T(128)} %constant.91.clone.1), window={size=4x1 pad=3_0x0_0}, to_apply=%region_5.6 | reduce-window | flops 2688 | bytes 7172 | tf_op jit(solution)/shard_map/jit(cumsum)/reduce_window_sum | solution.py:97
  23.6 0.7 %dynamic-slice_dynamic-update-slice_fusion = bf16[896,2240]{1,0:T(8,128)(2,1)} fusion(bf16[896,2240]{1,0:T(8,128)(2,1)} %dynamic-slice_dynamic-update-slice_fusion.1, bf16[224,2240]{1,0:T(8,128)(2,1)S(1)} %copy-done.2, s32[]{:T(128)S(6)} %select_n.84), kind=kLoop, calls=%fused_computation.45 | loop fusion | bytes 508932
  24.3 1.7 %collective-permute-start.1 = (bf16[56,2240]{1,0:T(8,128)(2,1)}, bf16[56,2240]{1,0:T(8,128)(2,1)S(1)}, u32[]{:S(2)}, u32[]{:S(2)}) collective-permute-start(bf16[56,2240]{1,0:T(8,128)(2,1)} %collective-permute-done), channel_id=1, source_target_pairs={{0,16},{16,0},{1,17},{17,1},{2,18},{18,2},{3,19},{19,3},{4,20},{20... | collective-permute-start | bytes 752648 | tf_op jit(solution)/shard_map/ppermute | solution.py:44
  26.0 1.9 %collective-permute-start.3 = (bf16[56,2240]{1,0:T(8,128)(2,1)}, bf16[56,2240]{1,0:T(8,128)(2,1)S(1)}, u32[]{:S(2)}, u32[]{:S(2)}) collective-permute-start(bf16[56,2240]{1,0:T(8,128)(2,1)} %collective-permute-done), channel_id=1, source_target_pairs={{0,4},{4,8},{8,12},{12,0},{1,5},{5,9},{9,13},{13,1},{2,6},{6,10},{... | collective-permute-start | bytes 752648 | tf_op jit(solution)/shard_map/ppermute | solution.py:42
  28.0 1.7 %constant_dynamic-update-slice_fusion.3 = bf16[896,2240]{1,0:T(8,128)(2,1)} fusion(bf16[896,2240]{1,0:T(8,128)(2,1)} %dynamic-slice_dynamic-update-slice_fusion, bf16[56,2240]{1,0:T(8,128)(2,1)} %collective-permute-done), kind=kLoop, calls=%fused_computation.62 | loop fusion | bytes 516096
  29.7 2.5 %collective-permute-done.1 = bf16[56,2240]{1,0:T(8,128)(2,1)S(1)} collective-permute-done((bf16[56,2240]{1,0:T(8,128)(2,1)}, bf16[56,2240]{1,0:T(8,128)(2,1)S(1)}, u32[]{:S(2)}, u32[]{:S(2)}) %collective-permute-start.1) | collective-permute-done | bytes 250912 | tf_op jit(solution)/shard_map/ppermute | solution.py:44
  32.2 1.8 %pad_maximum_fusion = bf16[2,56,2240]{2,1,0:T(8,128)(2,1)} fusion(bf16[1,56,2240]{2,1,0:T(8,128)(2,1)S(1)} %bitcast.84, bf16[1,56,2240]{2,1,0:T(8,128)(2,1)} %bitcast.10), kind=kLoop, calls=%fused_computation.22 | loop fusion | flops 250880 | bytes 1003520 | tf_op jit(solution)/shard_map/stack | solution.py:47
  34.0 3.5 %collective-permute-done.3 = bf16[56,2240]{1,0:T(8,128)(2,1)S(1)} collective-permute-done((bf16[56,2240]{1,0:T(8,128)(2,1)}, bf16[56,2240]{1,0:T(8,128)(2,1)S(1)}, u32[]{:S(2)}, u32[]{:S(2)}) %collective-permute-start.3) | collective-permute-done | bytes 250912 | tf_op jit(solution)/shard_map/ppermute | solution.py:42
  37.5 1.5 %collective-permute-start.4 = (bf16[56,2240]{1,0:T(8,128)(2,1)S(1)}, bf16[56,2240]{1,0:T(8,128)(2,1)S(1)}, u32[]{:S(2)}, u32[]{:S(2)}) collective-permute-start(bf16[56,2240]{1,0:T(8,128)(2,1)S(1)} %collective-permute-done.3), channel_id=1, source_target_pairs={{0,16},{16,0},{1,17},{17,1},{2,18},{18,2},{3,19},{19,3},{4,20},{20... | collective-permute-start | bytes 752648 | tf_op jit(solution)/shard_map/ppermute | solution.py:44
  41.4 1.6 %divide_convert_fusion = bf16[4,512,224]{1,2,0:T(8,128)(2,1)} fusion(f32[4,512,224]{1,2,0:T(8,128)S(1)} %fusion.11, bf16[28,4,8,512]{3,2,1,0:T(8,128)(2,1)S(1)} %bitcast.80, pred[224,224]{1,0:T(8,128)(4,1)S(1)} %broadcast_compare_fusion, bf16[4,224]{1,0:T(4,128)(2,1)S(1)} %copy.46), kind=kOutput, calls=%fused_computation.5 | convolution fusion | flops 207097856 | bytes 3721984 | tf_op jit(solution)/shard_map/fti,fij->ftj/dot_general | solution.py:105
  43.0 3.5 %all-to-all-start.1 = ((bf16[4,512,224]{1,2,0:T(8,128)(2,1)}), bf16[4,512,224]{1,2,0:T(8,128)(2,1)S(1)}, u32[]{:S(2)}, u32[]{:S(2)}) async-start(bf16[4,512,224]{1,2,0:T(8,128)(2,1)} %divide_convert_fusion), calls=%async_computation.1 | async-start | bytes 1835008 | tf_op jit(solution)/shard_map/all_to_all | solution.py:121
  47.2 1.7 %fusion.24 = bf16[896,2240]{1,0:T(8,128)(2,1)} fusion(bf16[896,2240]{1,0:T(8,128)(2,1)} %constant_dynamic-update-slice_fusion.2, bf16[2,56,2240]{2,1,0:T(8,128)(2,1)} %collective-permute-done.2), kind=kLoop, calls=%fused_computation.44 | loop fusion | bytes 516096
  48.8 1.7 %fusion.23 = bf16[896,2240]{1,0:T(8,128)(2,1)} fusion(bf16[896,2240]{1,0:T(8,128)(2,1)} %fusion.24, bf16[2,56,2240]{2,1,0:T(8,128)(2,1)} %collective-permute-done.2), kind=kLoop, calls=%fused_computation.42 | loop fusion | bytes 516096
  50.5 0.7 %constant_dynamic-update-slice_fusion.1 = bf16[896,2240]{1,0:T(8,128)(2,1)} fusion(bf16[896,2240]{1,0:T(8,128)(2,1)} %fusion.23, bf16[56,2240]{1,0:T(8,128)(2,1)S(1)} %collective-permute-done.3), kind=kLoop, calls=%fused_computation.60 | loop fusion | bytes 508928
  52.7 0.7 %fusion.21 = bf16[896,2240]{1,0:T(8,128)(2,1)} fusion(bf16[896,2240]{1,0:T(8,128)(2,1)} %fusion.22, bf16[2,56,2240]{2,1,0:T(8,128)(2,1)S(1)} %collective-permute-done.5), kind=kLoop, calls=%fused_computation.38 | loop fusion | bytes 508928
  53.4 1.7 %fusion.20 = bf16[896,2240]{1,0:T(8,128)(2,1)} fusion(bf16[896,2240]{1,0:T(8,128)(2,1)} %fusion.21, bf16[2,56,2240]{2,1,0:T(8,128)(2,1)} %collective-permute-done.6), kind=kLoop, calls=%fused_computation.36 | loop fusion | bytes 516096
  55.1 1.7 %fusion.19 = bf16[896,2240]{1,0:T(8,128)(2,1)} fusion(bf16[896,2240]{1,0:T(8,128)(2,1)} %fusion.20, bf16[2,56,2240]{2,1,0:T(8,128)(2,1)} %collective-permute-done.6), kind=kLoop, calls=%fused_computation.34 | loop fusion | bytes 516096
  56.8 1.7 %fusion.18 = bf16[896,2240]{1,0:T(8,128)(2,1)} fusion(bf16[896,2240]{1,0:T(8,128)(2,1)} %fusion.19, bf16[2,56,2240]{2,1,0:T(8,128)(2,1)} %collective-permute-done.7), kind=kLoop, calls=%fused_computation.32 | loop fusion | bytes 516096
  58.4 1.7 %fusion.17 = bf16[896,2240]{1,0:T(8,128)(2,1)} fusion(bf16[896,2240]{1,0:T(8,128)(2,1)} %fusion.18, bf16[2,56,2240]{2,1,0:T(8,128)(2,1)} %collective-permute-done.7), kind=kLoop, calls=%fused_computation.30 | loop fusion | bytes 516096 | tf_op jit(solution)/shard_map/concatenate | solution.py:52
  60.1 8.1 %fusion.1 = bf16[512,2240]{0,1:T(8,128)(2,1)} fusion(bf16[896,2240]{1,0:T(8,128)(2,1)} %fusion.17, bf16[512,2240]{0,1:T(8,128)(2,1)} %param.10, f32[2240]{0:T(1024)S(1)} %dynamic-slice_reduce_fusion, bf16[512,896]{0,1:T(8,128)(2,1)S(1)} %bitcast.85, s32[896]{0:T(1024)S(1)} %add.156), kind=kOutput, calls=%fused_computation.2 | convolution fusion | flops 2883141632 | bytes 9531648 | tf_op jit(solution)/shard_map/dot_general | solution.py:131
  (54 shorter events, 6.2 us)
Async XLA Ops:
  0.0 22.4 %copy-start = (f32[4,2240]{1,0:T(4,128)S(1)}, f32[4,2240]{1,0:T(4,128)}, u32[]{:S(2)}) copy-start(f32[4,2240]{1,0:T(4,128)} %param.12) | copy-start | bytes 107524
  0.0 11.7 %copy-start.1 = (bf16[2048,224]{0,1:T(8,128)(2,1)S(1)}, bf16[2048,224]{0,1:T(8,128)(2,1)}, u32[]{:S(2)}) copy-start(bf16[2048,224]{0,1:T(8,128)(2,1)} %param.8) | copy-start | bytes 2752516
  0.0 12.1 %copy-start.4 = (bf16[2048,224]{0,1:T(8,128)(2,1)S(1)}, bf16[2048,224]{0,1:T(8,128)(2,1)}, u32[]{:S(2)}) copy-start(bf16[2048,224]{0,1:T(8,128)(2,1)} %param.9) | copy-start | bytes 2752516
  1.9 22.4 %collective-permute-start = (bf16[56,2240]{1,0:T(8,128)(2,1)}, bf16[56,2240]{1,0:T(8,128)(2,1)}, u32[]{:S(2)}, u32[]{:S(2)}) collective-permute-start(bf16[56,2240]{1,0:T(8,128)(2,1)} %get-tuple-element.6), channel_id=1, source_target_pairs={{0,4},{4,8},{8,12},{12,0},{1,5},{5,9},{9,13},{13,1},{2,6},{6,10},{... | collective-permute-start | bytes 752648 | tf_op jit(solution)/shard_map/ppermute | solution.py:42
  8.5 30.6 %collective-permute-start.6 = (bf16[2,56,2240]{2,1,0:T(8,128)(2,1)}, bf16[2,56,2240]{2,1,0:T(8,128)(2,1)}, u32[]{:S(2)}, u32[]{:S(2)}) collective-permute-start(bf16[2,56,2240]{2,1,0:T(8,128)(2,1)} %pad_maximum_fusion.2), channel_id=1, source_target_pairs={{0,12},{4,0},{8,4},{12,8},{1,13},{5,1},{9,5},{13,9},{2,14},{6,2},{... | collective-permute-start | bytes 1505288 | tf_op jit(solution)/shard_map/ppermute | solution.py:38
  12.0 6.9 %copy-start.5 = (s32[4]{0:T(128)S(1)}, s32[4]{0:T(128)}, u32[]{:S(2)}) copy-start(s32[4]{0:T(128)} %constant.99.clone) | copy-start | bytes 52
  13.5 8.1 %copy-start.2 = (bf16[224,2240]{1,0:T(8,128)(2,1)S(1)}, bf16[224,2240]{1,0:T(8,128)(2,1)}, u32[]{:S(2)}) copy-start(bf16[224,2240]{1,0:T(8,128)(2,1)} %param.11) | copy-start | bytes 3010564
  14.7 25.1 %all-to-all-start = ((f32[4,2,113,112]{2,3,1,0:T(8,128)}), f32[4,2,113,112]{2,3,1,0:T(8,128)S(1)}, u32[]{:S(2)}, u32[]{:S(2)}) async-start(f32[4,2,113,112]{2,3,1,0:T(8,128)} %broadcast_select_fusion), calls=%async_computation | async-start | bytes 917504 | tf_op jit(solution)/shard_map/all_to_all | solution.py:19
  21.7 19.1 %copy-start.3 = (f32[4,224,224]{2,1,0:T(8,128)S(1)}, f32[4,224,224]{2,1,0:T(8,128)}, u32[]{:S(2)}) copy-start(f32[4,224,224]{2,1,0:T(8,128)} %get-tuple-element.12) | copy-start | bytes 2408452
  24.3 7.9 %collective-permute-start.1 = (bf16[56,2240]{1,0:T(8,128)(2,1)}, bf16[56,2240]{1,0:T(8,128)(2,1)S(1)}, u32[]{:S(2)}, u32[]{:S(2)}) collective-permute-start(bf16[56,2240]{1,0:T(8,128)(2,1)} %collective-permute-done), channel_id=1, source_target_pairs={{0,16},{16,0},{1,17},{17,1},{2,18},{18,2},{3,19},{19,3},{4,20},{20... | collective-permute-start | bytes 752648 | tf_op jit(solution)/shard_map/ppermute | solution.py:44
  26.0 11.5 %collective-permute-start.3 = (bf16[56,2240]{1,0:T(8,128)(2,1)}, bf16[56,2240]{1,0:T(8,128)(2,1)S(1)}, u32[]{:S(2)}, u32[]{:S(2)}) collective-permute-start(bf16[56,2240]{1,0:T(8,128)(2,1)} %collective-permute-done), channel_id=1, source_target_pairs={{0,4},{4,8},{8,12},{12,0},{1,5},{5,9},{9,13},{13,1},{2,6},{6,10},{... | collective-permute-start | bytes 752648 | tf_op jit(solution)/shard_map/ppermute | solution.py:42
  34.0 13.2 %collective-permute-start.2 = (bf16[2,56,2240]{2,1,0:T(8,128)(2,1)}, bf16[2,56,2240]{2,1,0:T(8,128)(2,1)}, u32[]{:S(2)}, u32[]{:S(2)}) collective-permute-start(bf16[2,56,2240]{2,1,0:T(8,128)(2,1)} %pad_maximum_fusion), channel_id=1, source_target_pairs={{0,1},{1,0},{2,3},{3,2},{4,5},{5,4},{6,7},{7,6},{8,9},{9,8},{10,11... | collective-permute-start | bytes 1505288 | tf_op jit(solution)/shard_map/ppermute | solution.py:47
  37.5 9.1 %collective-permute-start.4 = (bf16[56,2240]{1,0:T(8,128)(2,1)S(1)}, bf16[56,2240]{1,0:T(8,128)(2,1)S(1)}, u32[]{:S(2)}, u32[]{:S(2)}) collective-permute-start(bf16[56,2240]{1,0:T(8,128)(2,1)S(1)} %collective-permute-done.3), channel_id=1, source_target_pairs={{0,16},{16,0},{1,17},{17,1},{2,18},{18,2},{3,19},{19,3},{4,20},{20... | collective-permute-start | bytes 752648 | tf_op jit(solution)/shard_map/ppermute | solution.py:44
  39.0 17.7 %collective-permute-start.7 = (bf16[2,56,2240]{2,1,0:T(8,128)(2,1)}, bf16[2,56,2240]{2,1,0:T(8,128)(2,1)}, u32[]{:S(2)}, u32[]{:S(2)}) collective-permute-start(bf16[2,56,2240]{2,1,0:T(8,128)(2,1)} %collective-permute-done.6), channel_id=1, source_target_pairs={{0,1},{1,0},{2,3},{3,2},{4,5},{5,4},{6,7},{7,6},{8,9},{9,8},{10,11... | collective-permute-start | bytes 1505288 | tf_op jit(solution)/shard_map/ppermute | solution.py:50
  43.0 17.1 %all-to-all-start.1 = ((bf16[4,512,224]{1,2,0:T(8,128)(2,1)}), bf16[4,512,224]{1,2,0:T(8,128)(2,1)S(1)}, u32[]{:S(2)}, u32[]{:S(2)}) async-start(bf16[4,512,224]{1,2,0:T(8,128)(2,1)} %divide_convert_fusion), calls=%async_computation.1 | async-start | bytes 1835008 | tf_op jit(solution)/shard_map/all_to_all | solution.py:121
  46.6 5.3 %collective-permute-start.5 = (bf16[2,56,2240]{2,1,0:T(8,128)(2,1)S(1)}, bf16[2,56,2240]{2,1,0:T(8,128)(2,1)S(1)}, u32[]{:S(2)}, u32[]{:S(2)}) collective-permute-start(bf16[2,56,2240]{2,1,0:T(8,128)(2,1)S(1)} %pad_maximum_fusion.1), channel_id=1, source_target_pairs={{0,1},{1,0},{2,3},{3,2},{4,5},{5,4},{6,7},{7,6},{8,9},{9,8},{10,11... | collective-permute-start | bytes 1505288 | tf_op jit(solution)/shard_map/ppermute | solution.py:47

commit v4 on v2

--- a/solution.py
+++ b/solution.py
@@ -116,9 +116,15 @@
     block = jnp.remainder(j - jnp.arange(nf, dtype=jnp.int32), nf)
     order = (block[:, None] * nparts + shares[None, :]).reshape(-1)
     source = (order[:, None] * sub + jnp.arange(sub, dtype=jnp.int32)[None, :]).reshape(-1)
-    pick = (jnp.arange(depth, dtype=jnp.int32)[:, None] == source[None, :]).astype(jnp.bfloat16)
-    matched = jnp.dot(token_rows, pick, preferred_element_type=jnp.float32).astype(jnp.bfloat16)
-    projected = jnp.dot(matched, weights, preferred_element_type=jnp.float32)
+    columns = jnp.arange(depth, dtype=jnp.int32)[:, None]
+    split = (nf - 1) * nparts * sub
+
+    def part(lo, hi):
+        pick = (columns == source[None, lo:hi]).astype(jnp.bfloat16)
+        matched = jnp.dot(token_rows, pick, preferred_element_type=jnp.float32).astype(jnp.bfloat16)
+        return jnp.dot(matched, weights[lo:hi], preferred_element_type=jnp.float32)
+
+    projected = part(0, split) + part(split, depth)
     return (residual.astype(jnp.float32) + gate_rows * projected).astype(jnp.bfloat16)
 
 

time: 67.2 us -> 69.4 us (1.033)
  matrix products: 12.8 us -> 16.2 us
  waiting for transfers between devices: 13 us -> 11.6 us
  other arithmetic: 8.46 us -> 9.6 us
  local copies, waits for them, and re-layouts: 15.4 us -> 14.6 us
    dot_general x1 -> x2, matrix products: 8.07 us -> 12.7 us  [part(): return jnp.dot(matched, weights[lo:hi], preferred_element_type=jnp.float32)]
    unnamed x19 -> x29, local copies, waits for them, and re-layouts: 13 us -> 10.2 us
    squeeze x0 -> x1, local copies, waits for them, and re-layouts: none -> 1.95 us  [_ring_out_proj(): pieces += from_groups + [from_core[s] for s in range(ng)]]
    another operation x3, other arithmetic: 1.09 us -> 2.76 us  [_ring_out_proj(): from_core = lax.ppermute(jnp.stack(from_groups), 'heads', swap)]
    ppermute x3, waiting for transfers between devices: 2.87 us -> 1.48 us  [_ring_out_proj(): piece = lax.ppermute(piece, 'frames', ring)]
    dot_general x1, matrix products: 2.57 us -> 1.38 us  [_attend(): jnp.einsum('fti,ftj->fij', key_pos, value_frames, preferred_element_type=...]
    reduce_sum x1, other arithmetic: 1.44 us -> 0.26 us  [_attend(): own_sum = jnp.sum(frame_sum, axis=0)]
  transfers between devices with their start and end apart: 11 -> 11, of which waited for: 3 -> 3; matrix products, arithmetic and copies ran while one was open for 40% -> 45% of each run, Pallas kernels for 0% -> 0%
where the time goes in v4:
time: 69.4 us; the launch traced here: 68.8 us
  starting transfers between devices  16.5 us (24%)
  matrix products  16.2 us (23%)
  local copies, waits for them, and re-layouts  14.6 us (21%)
  waiting for transfers between devices  11.6 us (17%)
  other arithmetic  9.6 us (14%)
    dot_general x2, matrix products, part(): return jnp.dot(matched, weights[lo:hi], preferred_element_type=jnp.float32)  12.7 us
    unnamed x29, local copies, waits for them, and re-layouts  10.2 us
    ppermute x3, waiting for transfers between devices, _ring_out_proj(): lax.ppermute(piece, 'groups', [(a, (a + s) % ng) for a in range(ng)])  10.1 us
    ppermute x3, starting transfers between devices, _ring_out_proj(): piece = lax.ppermute(piece, 'frames', ring)  5.38 us
    all_to_all x1, starting transfers between devices, _exclusive_prefix(): lax.all_to_all(outgoing, 'frames', split_axis=0, concat_axis=0, tiled=True)  3.86 us
    ppermute x3, starting transfers between devices, _ring_out_proj(): lax.ppermute(piece, 'groups', [(a, (a + s) % ng) for a in range(ng)])  3.62 us
    all_to_all x1, starting transfers between devices, _project(): lax.all_to_all(attended, 'heads', split_axis=0, concat_axis=1, tiled=True)  3.51 us
    another operation x3, other arithmetic, _ring_out_proj(): from_core = lax.ppermute(jnp.stack(from_groups), 'heads', swap)  2.76 us
  transfers between devices with their start and end apart: 11, of which 3 were waited for; matrix products, arithmetic and copies ran while one was open for 45% of the time, Pallas kernels for 0%

profile of v4, /device:TPU:0, one launch (start us, length us, event | category | flops | bytes accessed | tf_op | source)
XLA Modules:
  0.0 68.8 jit_solution(16728546497597122470)
XLA Ops:
  0.0 1.9 %constant_dynamic-update-slice_fusion.4 = (bf16[672,2240]{1,0:T(8,128)(2,1)}, bf16[56,2240]{1,0:T(8,128)(2,1)}) fusion(bf16[224,2240]{1,0:T(8,128)(2,1)} %param.10, s32[]{:T(128)S(6)} %select_n.85), kind=kLoop, calls=%fused_computation.68 | loop fusion | bytes 766980
  1.9 3.1 %collective-permute-start = (bf16[56,2240]{1,0:T(8,128)(2,1)}, bf16[56,2240]{1,0:T(8,128)(2,1)}, u32[]{:S(2)}, u32[]{:S(2)}) collective-permute-start(bf16[56,2240]{1,0:T(8,128)(2,1)} %get-tuple-element.6), channel_id=1, source_target_pairs={{0,4},{4,8},{8,12},{12,0},{1,5},{5,9},{9,13},{13,1},{2,6},{6,10},{... | collective-permute-start | bytes 752648 | tf_op jit(solution)/shard_map/ppermute | solution.py:35
  5.0 1.2 %broadcast_maximum_fusion = bf16[2048,224]{0,1:T(8,128)(2,1)S(1)} fusion(bf16[2048,224]{0,1:T(8,128)(2,1)} %param.7), kind=kLoop, calls=%fused_computation.38 | loop fusion | flops 458752 | bytes 1835008 | tf_op jit(solution)/shard_map/max | solution.py:60
  6.7 1.4 %fusion.38 = (f32[224,224]{1,0:T(8,128)S(1)}, f32[4,224,224]{2,1,0:T(8,128)}) fusion(bf16[28,4,8,512]{3,2,1,0:T(8,128)(2,1)S(1)} %bitcast.80, bf16[28,4,8,512]{3,2,1,0:T(8,128)(2,1)S(1)} %bitcast.69, pred[224,224]{1,0:T(8,128)(4,1)S(1)} %broadcast_compare_fusion), kind=kOutput, calls=%fused_computation.87 | convolution fusion | flops 205872128 | bytes 2888704 | tf_op jit(solution)/shard_map/fti,ftj->fij/dot_general | solution.py:65
  8.4 0.9 %broadcast_select_fusion = f32[4,2,113,112]{2,3,1,0:T(8,128)} fusion(f32[2,113,112]{1,2,0:T(8,128)S(1)} %copy.41, pred[4]{0:T(512)(128)(4,1)S(1)} %iota_compare_fusion.9), kind=kLoop, calls=%fused_computation.57 | loop fusion | flops 101248 | bytes 506244 | tf_op jit(solution)/shard_map/jit(_where)/select_n | solution.py:16
  9.2 3.9 %all-to-all-start = ((f32[4,2,113,112]{2,3,1,0:T(8,128)}), f32[4,2,113,112]{2,3,1,0:T(8,128)S(1)}, u32[]{:S(2)}, u32[]{:S(2)}) async-start(f32[4,2,113,112]{2,3,1,0:T(8,128)} %broadcast_select_fusion), calls=%async_computation | async-start | bytes 917504 | tf_op jit(solution)/shard_map/all_to_all | solution.py:19
  14.2 1.2 %broadcast_maximum_fusion.1 = bf16[2048,224]{0,1:T(8,128)(2,1)S(1)} fusion(bf16[2048,224]{0,1:T(8,128)(2,1)} %param.6), kind=kLoop, calls=%fused_computation.39 | loop fusion | flops 458752 | bytes 1835008 | tf_op jit(solution)/shard_map/max | solution.py:59
  16.0 0.7 %dynamic-slice_dynamic-update-slice_fusion.2 = bf16[672,2240]{1,0:T(8,128)(2,1)} fusion(bf16[672,2240]{1,0:T(8,128)(2,1)} %get-tuple-element.5, bf16[224,2240]{1,0:T(8,128)(2,1)S(1)} %copy-done.3, s32[]{:T(128)S(6)} %select_n.86), kind=kLoop, calls=%fused_computation.53 | loop fusion | bytes 508932
  16.7 0.7 %dynamic-slice_dynamic-update-slice_fusion.1 = bf16[672,2240]{1,0:T(8,128)(2,1)} fusion(bf16[672,2240]{1,0:T(8,128)(2,1)} %dynamic-slice_dynamic-update-slice_fusion.2, bf16[224,2240]{1,0:T(8,128)(2,1)S(1)} %copy-done.3, s32[]{:T(128)S(6)} %select_n.87), kind=kLoop, calls=%fused_computation.52 | loop fusion | bytes 508932
  17.4 0.8 %reduce_window_sum.23 = f32[4,224]{0,1:T(8,128)} reduce-window(f32[4,224]{0,1:T(8,128)S(1)} %convert_reduce_fusion, f32[]{:T(128)} %constant.89.clone.1), window={size=4x1 pad=3_0x0_0}, to_apply=%region_5.6 | reduce-window | flops 2688 | bytes 7172 | tf_op jit(solution)/shard_map/jit(cumsum)/reduce_window_sum | solution.py:87
  18.3 0.7 %dynamic-slice_dynamic-update-slice_fusion = bf16[672,2240]{1,0:T(8,128)(2,1)} fusion(bf16[672,2240]{1,0:T(8,128)(2,1)} %dynamic-slice_dynamic-update-slice_fusion.1, bf16[224,2240]{1,0:T(8,128)(2,1)S(1)} %copy-done.3, s32[]{:T(128)S(6)} %select_n.88), kind=kLoop, calls=%fused_computation.51 | loop fusion | bytes 508932
  19.1 1.5 %collective-permute-start.1 = (bf16[56,2240]{1,0:T(8,128)(2,1)}, bf16[56,2240]{1,0:T(8,128)(2,1)S(1)}, u32[]{:S(2)}, u32[]{:S(2)}) collective-permute-start(bf16[56,2240]{1,0:T(8,128)(2,1)} %collective-permute-done), channel_id=1, source_target_pairs={{0,16},{16,0},{1,17},{17,1},{2,18},{18,2},{3,19},{19,3},{4,20},{20... | collective-permute-start | bytes 752648 | tf_op jit(solution)/shard_map/ppermute | solution.py:37
  20.6 2.0 %collective-permute-start.3 = (bf16[56,2240]{1,0:T(8,128)(2,1)}, bf16[56,2240]{1,0:T(8,128)(2,1)S(1)}, u32[]{:S(2)}, u32[]{:S(2)}) collective-permute-start(bf16[56,2240]{1,0:T(8,128)(2,1)} %collective-permute-done), channel_id=1, source_target_pairs={{0,4},{4,8},{8,12},{12,0},{1,5},{5,9},{9,13},{13,1},{2,6},{6,10},{... | collective-permute-start | bytes 752648 | tf_op jit(solution)/shard_map/ppermute | solution.py:35
  22.6 1.7 %constant_dynamic-update-slice_fusion.3 = bf16[672,2240]{1,0:T(8,128)(2,1)} fusion(bf16[672,2240]{1,0:T(8,128)(2,1)} %dynamic-slice_dynamic-update-slice_fusion, bf16[56,2240]{1,0:T(8,128)(2,1)} %collective-permute-done), kind=kLoop, calls=%fused_computation.67 | loop fusion | bytes 516096
  24.3 2.4 %collective-permute-done.1 = bf16[56,2240]{1,0:T(8,128)(2,1)S(1)} collective-permute-done((bf16[56,2240]{1,0:T(8,128)(2,1)}, bf16[56,2240]{1,0:T(8,128)(2,1)S(1)}, u32[]{:S(2)}, u32[]{:S(2)}) %collective-permute-start.1) | collective-permute-done | bytes 250912 | tf_op jit(solution)/shard_map/ppermute | solution.py:37
  26.7 1.8 %pad_maximum_fusion = bf16[2,56,2240]{2,1,0:T(8,128)(2,1)} fusion(bf16[1,56,2240]{2,1,0:T(8,128)(2,1)S(1)} %bitcast.77, bf16[1,56,2240]{2,1,0:T(8,128)(2,1)} %bitcast.10), kind=kLoop, calls=%fused_computation.33 | loop fusion | flops 250880 | bytes 1003520 | tf_op jit(solution)/shard_map/stack | solution.py:40
  28.4 1.5 %collective-permute-done.3 = bf16[56,2240]{1,0:T(8,128)(2,1)S(1)} collective-permute-done((bf16[56,2240]{1,0:T(8,128)(2,1)}, bf16[56,2240]{1,0:T(8,128)(2,1)S(1)}, u32[]{:S(2)}, u32[]{:S(2)}) %collective-permute-start.3) | collective-permute-done | bytes 250912 | tf_op jit(solution)/shard_map/ppermute | solution.py:35
  29.9 1.5 %collective-permute-start.4 = (bf16[56,2240]{1,0:T(8,128)(2,1)S(1)}, bf16[56,2240]{1,0:T(8,128)(2,1)S(1)}, u32[]{:S(2)}, u32[]{:S(2)}) collective-permute-start(bf16[56,2240]{1,0:T(8,128)(2,1)S(1)} %collective-permute-done.3), channel_id=1, source_target_pairs={{0,16},{16,0},{1,17},{17,1},{2,18},{18,2},{3,19},{19,3},{4,20},{20... | collective-permute-start | bytes 752648 | tf_op jit(solution)/shard_map/ppermute | solution.py:37
  31.7 0.7 %constant_dynamic-update-slice_fusion.2 = bf16[672,2240]{1,0:T(8,128)(2,1)} fusion(bf16[672,2240]{1,0:T(8,128)(2,1)} %constant_dynamic-update-slice_fusion.3, bf16[56,2240]{1,0:T(8,128)(2,1)S(1)} %collective-permute-done.1), kind=kLoop, calls=%fused_computation.66 | loop fusion | bytes 508928
  33.4 1.3 %fusion.6 = bf16[4,224,224]{2,1,0:T(8,128)(2,1)S(1)} fusion(f32[4,224,224]{2,1,0:T(8,128)} %get-tuple-element.12, f32[224,224]{1,0:T(8,128)S(1)} %add.129), kind=kOutput, calls=%fused_computation.13 | output fusion | flops 1003520 | bytes 1404928 | tf_op jit(solution)/shard_map/jit(cumsum)/reduce_window_sum | solution.py:86
  35.2 1.6 %divide_convert_fusion = bf16[4,512,224]{1,2,0:T(8,128)(2,1)} fusion(f32[4,512,224]{1,2,0:T(8,128)S(1)} %fusion.19, bf16[28,4,8,512]{3,2,1,0:T(8,128)(2,1)S(1)} %bitcast.71, pred[224,224]{1,0:T(8,128)(4,1)S(1)} %copy-done.7, bf16[4,224]{1,0:T(4,128)(2,1)S(1)} %copy.45), kind=kOutput, calls=%fused_computation.6 | convolution fusion | flops 207097856 | bytes 3721984 | tf_op jit(solution)/shard_map/fti,fij->ftj/dot_general | solution.py:95
  36.8 3.5 %all-to-all-start.1 = ((bf16[4,512,224]{1,2,0:T(8,128)(2,1)}), bf16[4,512,224]{1,2,0:T(8,128)(2,1)S(1)}, u32[]{:S(2)}, u32[]{:S(2)}) async-start(bf16[4,512,224]{1,2,0:T(8,128)(2,1)} %divide_convert_fusion), calls=%async_computation.1 | async-start | bytes 1835008 | tf_op jit(solution)/shard_map/all_to_all | solution.py:111
  41.2 7.8 %collective-permute-done.7 = bf16[56,2240]{1,0:T(8,128)(2,1)S(1)} collective-permute-done((bf16[56,2240]{1,0:T(8,128)(2,1)S(1)}, bf16[56,2240]{1,0:T(8,128)(2,1)S(1)}, u32[]{:S(2)}, u32[]{:S(2)}) %collective-permute-start.7) | collective-permute-done | bytes 250912 | tf_op jit(solution)/shard_map/ppermute | solution.py:37
  48.9 0.9 %pad_maximum_fusion.2 = bf16[2,56,2240]{2,1,0:T(8,128)(2,1)} fusion(bf16[1,56,2240]{2,1,0:T(8,128)(2,1)S(1)} %bitcast.73, bf16[1,56,2240]{2,1,0:T(8,128)(2,1)S(1)} %bitcast.72), kind=kLoop, calls=%fused_computation.35 | loop fusion | flops 250880 | bytes 1003520 | tf_op jit(solution)/shard_map/stack | solution.py:40
  49.9 0.7 %fusion.31 = bf16[672,2240]{1,0:T(8,128)(2,1)} fusion(bf16[672,2240]{1,0:T(8,128)(2,1)} %constant_dynamic-update-slice_fusion.2, bf16[2,56,2240]{2,1,0:T(8,128)(2,1)S(1)} %collective-permute-done.2), kind=kLoop, calls=%fused_computation.50 | loop fusion | bytes 508928
  50.6 0.7 %fusion.30 = bf16[672,2240]{1,0:T(8,128)(2,1)} fusion(bf16[672,2240]{1,0:T(8,128)(2,1)} %fusion.31, bf16[2,56,2240]{2,1,0:T(8,128)(2,1)S(1)} %collective-permute-done.2), kind=kLoop, calls=%fused_computation.48 | loop fusion | bytes 508928
  51.3 0.7 %constant_dynamic-update-slice_fusion.1 = bf16[672,2240]{1,0:T(8,128)(2,1)} fusion(bf16[672,2240]{1,0:T(8,128)(2,1)} %fusion.30, bf16[56,2240]{1,0:T(8,128)(2,1)S(1)} %collective-permute-done.3), kind=kLoop, calls=%fused_computation.65 | loop fusion | bytes 508928
  52.0 0.7 %constant_dynamic-update-slice_fusion = bf16[672,2240]{1,0:T(8,128)(2,1)} fusion(bf16[672,2240]{1,0:T(8,128)(2,1)} %constant_dynamic-update-slice_fusion.1, bf16[56,2240]{1,0:T(8,128)(2,1)S(1)} %collective-permute-done.4), kind=kLoop, calls=%fused_computation.64 | loop fusion | bytes 508928
  52.7 0.7 %fusion.29 = bf16[672,2240]{1,0:T(8,128)(2,1)} fusion(bf16[672,2240]{1,0:T(8,128)(2,1)} %constant_dynamic-update-slice_fusion, bf16[2,56,2240]{2,1,0:T(8,128)(2,1)S(1)} %collective-permute-done.5), kind=kLoop, calls=%fused_computation.46 | loop fusion | bytes 508928
  54.2 7.0 %fusion.23 = f32[512,2240]{0,1:T(8,128)} fusion(bf16[672,2240]{1,0:T(8,128)(2,1)} %fusion.28, bf16[512,896]{0,1:T(8,128)(2,1)S(1)} %bitcast.67, s32[672]{0:T(1024)S(1)} %eq.69), kind=kOutput, calls=%fused_computation.32 | convolution fusion | flops 2158915584 | bytes 8518272 | tf_op jit(solution)/shard_map/dot_general | solution.py:125
  61.2 1.9 %slice_bitcast_fusion.1 = (bf16[56,2240]{1,0:T(8,128)(2,1)}, bf16[56,2240]{1,0:T(8,128)(2,1)}) fusion(bf16[2,56,2240]{2,1,0:T(8,128)(2,1)} %collective-permute-done.8), kind=kLoop, calls=%fused_computation.42 | loop fusion | bytes 1003520 | tf_op jit(solution)/shard_map/squeeze | solution.py:41
  63.1 5.7 %fusion.2 = bf16[512,2240]{0,1:T(8,128)(2,1)} fusion(f32[512,2240]{0,1:T(8,128)} %fusion.23, bf16[512,2240]{0,1:T(8,128)(2,1)S(1)} %copy-done.2, f32[2240]{0:T(1024)S(1)} %dynamic-slice_reduce_fusion, bf16[512,896]{0,1:T(8,128)(2,1)S(1)} %bitcast.68, bf16[56,2240]{1,0:T(8,128)(2,1)} %get-tuple-element.8, bf16[56,2240]{1,0:T(8,128)(2,1)} %get-tuple-element.7, ...), kind=kOutput, calls=%fused_computation.3 | convolution fusion | flops 729387008 | bytes 11105920 | tf_op jit(solution)/shard_map/dot_general | solution.py:125
  (62 shorter events, 5.5 us)
Async XLA Ops:
  0.0 18.3 %copy-start = (f32[4,2240]{1,0:T(4,128)S(1)}, f32[4,2240]{1,0:T(4,128)}, u32[]{:S(2)}) copy-start(f32[4,2240]{1,0:T(4,128)} %param.11) | copy-start | bytes 107524
  0.0 6.3 %copy-start.1 = (bf16[2048,224]{0,1:T(8,128)(2,1)S(1)}, bf16[2048,224]{0,1:T(8,128)(2,1)}, u32[]{:S(2)}) copy-start(bf16[2048,224]{0,1:T(8,128)(2,1)} %param.7) | copy-start | bytes 2752516
  0.0 6.7 %copy-start.8 = (bf16[2048,224]{0,1:T(8,128)(2,1)S(1)}, bf16[2048,224]{0,1:T(8,128)(2,1)}, u32[]{:S(2)}) copy-start(bf16[2048,224]{0,1:T(8,128)(2,1)} %param.8) | copy-start | bytes 2752516
  1.9 17.1 %collective-permute-start = (bf16[56,2240]{1,0:T(8,128)(2,1)}, bf16[56,2240]{1,0:T(8,128)(2,1)}, u32[]{:S(2)}, u32[]{:S(2)}) collective-permute-start(bf16[56,2240]{1,0:T(8,128)(2,1)} %get-tuple-element.6), channel_id=1, source_target_pairs={{0,4},{4,8},{8,12},{12,0},{1,5},{5,9},{9,13},{13,1},{2,6},{6,10},{... | collective-permute-start | bytes 752648 | tf_op jit(solution)/shard_map/ppermute | solution.py:35
  6.7 1.4 %copy-start.6 = (pred[224,224]{1,0:T(8,128)(4,1)}, pred[224,224]{1,0:T(8,128)(4,1)S(1)}, u32[]{:S(2)}) copy-start(pred[224,224]{1,0:T(8,128)(4,1)S(1)} %broadcast_compare_fusion) | copy-start | bytes 150532
  8.4 7.6 %copy-start.3 = (bf16[224,2240]{1,0:T(8,128)(2,1)S(1)}, bf16[224,2240]{1,0:T(8,128)(2,1)}, u32[]{:S(2)}) copy-start(bf16[224,2240]{1,0:T(8,128)(2,1)} %param.10) | copy-start | bytes 3010564
  9.2 23.2 %all-to-all-start = ((f32[4,2,113,112]{2,3,1,0:T(8,128)}), f32[4,2,113,112]{2,3,1,0:T(8,128)S(1)}, u32[]{:S(2)}, u32[]{:S(2)}) async-start(f32[4,2,113,112]{2,3,1,0:T(8,128)} %broadcast_select_fusion), calls=%async_computation | async-start | bytes 917504 | tf_op jit(solution)/shard_map/all_to_all | solution.py:19
  19.1 14.1 %copy-start.5 = (f32[4,224]{0,1:T(8,128)S(1)}, f32[4,224]{0,1:T(8,128)}, u32[]{:S(2)}) copy-start(f32[4,224]{0,1:T(8,128)} %reduce_window_sum.23) | copy-start | bytes 10756
  19.1 7.6 %collective-permute-start.1 = (bf16[56,2240]{1,0:T(8,128)(2,1)}, bf16[56,2240]{1,0:T(8,128)(2,1)S(1)}, u32[]{:S(2)}, u32[]{:S(2)}) collective-permute-start(bf16[56,2240]{1,0:T(8,128)(2,1)} %collective-permute-done), channel_id=1, source_target_pairs={{0,16},{16,0},{1,17},{17,1},{2,18},{18,2},{3,19},{19,3},{4,20},{20... | collective-permute-start | bytes 752648 | tf_op jit(solution)/shard_map/ppermute | solution.py:37
  20.6 9.3 %collective-permute-start.3 = (bf16[56,2240]{1,0:T(8,128)(2,1)}, bf16[56,2240]{1,0:T(8,128)(2,1)S(1)}, u32[]{:S(2)}, u32[]{:S(2)}) collective-permute-start(bf16[56,2240]{1,0:T(8,128)(2,1)} %collective-permute-done), channel_id=1, source_target_pairs={{0,4},{4,8},{8,12},{12,0},{1,5},{5,9},{9,13},{13,1},{2,6},{6,10},{... | collective-permute-start | bytes 752648 | tf_op jit(solution)/shard_map/ppermute | solution.py:35
  28.4 21.4 %collective-permute-start.2 = (bf16[2,56,2240]{2,1,0:T(8,128)(2,1)}, bf16[2,56,2240]{2,1,0:T(8,128)(2,1)S(1)}, u32[]{:S(2)}, u32[]{:S(2)}) collective-permute-start(bf16[2,56,2240]{2,1,0:T(8,128)(2,1)} %pad_maximum_fusion), channel_id=1, source_target_pairs={{0,1},{1,0},{2,3},{3,2},{4,5},{5,4},{6,7},{7,6},{8,9},{9,8},{10,11... | collective-permute-start | bytes 1505288 | tf_op jit(solution)/shard_map/ppermute | solution.py:40
  29.9 11.0 %collective-permute-start.4 = (bf16[56,2240]{1,0:T(8,128)(2,1)S(1)}, bf16[56,2240]{1,0:T(8,128)(2,1)S(1)}, u32[]{:S(2)}, u32[]{:S(2)}) collective-permute-start(bf16[56,2240]{1,0:T(8,128)(2,1)S(1)} %collective-permute-done.3), channel_id=1, source_target_pairs={{0,16},{16,0},{1,17},{17,1},{2,18},{18,2},{3,19},{19,3},{4,20},{20... | collective-permute-start | bytes 752648 | tf_op jit(solution)/shard_map/ppermute | solution.py:37
  31.4 8.9 %collective-permute-start.6 = (bf16[56,2240]{1,0:T(8,128)(2,1)S(1)}, bf16[56,2240]{1,0:T(8,128)(2,1)S(1)}, u32[]{:S(2)}, u32[]{:S(2)}) collective-permute-start(bf16[56,2240]{1,0:T(8,128)(2,1)S(1)} %collective-permute-done.3), channel_id=1, source_target_pairs={{0,4},{4,8},{8,12},{12,0},{1,5},{5,9},{9,13},{13,1},{2,6},{6,10},{... | collective-permute-start | bytes 752648 | tf_op jit(solution)/shard_map/ppermute | solution.py:35
  32.5 2.7 %copy-start.7 = (pred[224,224]{1,0:T(8,128)(4,1)S(1)}, pred[224,224]{1,0:T(8,128)(4,1)}, u32[]{:S(2)}) copy-start(pred[224,224]{1,0:T(8,128)(4,1)} %copy-done.6) | copy-start | bytes 150532
  36.8 17.4 %all-to-all-start.1 = ((bf16[4,512,224]{1,2,0:T(8,128)(2,1)}), bf16[4,512,224]{1,2,0:T(8,128)(2,1)S(1)}, u32[]{:S(2)}, u32[]{:S(2)}) async-start(bf16[4,512,224]{1,2,0:T(8,128)(2,1)} %divide_convert_fusion), calls=%async_computation.1 | async-start | bytes 1835008 | tf_op jit(solution)/shard_map/all_to_all | solution.py:111
  40.3 8.6 %collective-permute-start.7 = (bf16[56,2240]{1,0:T(8,128)(2,1)S(1)}, bf16[56,2240]{1,0:T(8,128)(2,1)S(1)}, u32[]{:S(2)}, u32[]{:S(2)}) collective-permute-start(bf16[56,2240]{1,0:T(8,128)(2,1)S(1)} %collective-permute-done.6), channel_id=1, source_target_pairs={{0,16},{16,0},{1,17},{17,1},{2,18},{18,2},{3,19},{19,3},{4,20},{20... | collective-permute-start | bytes 752648 | tf_op jit(solution)/shard_map/ppermute | solution.py:37
  41.0 11.8 %collective-permute-start.5 = (bf16[2,56,2240]{2,1,0:T(8,128)(2,1)S(1)}, bf16[2,56,2240]{2,1,0:T(8,128)(2,1)S(1)}, u32[]{:S(2)}, u32[]{:S(2)}) collective-permute-start(bf16[2,56,2240]{2,1,0:T(8,128)(2,1)S(1)} %pad_maximum_fusion.1), channel_id=1, source_target_pairs={{0,1},{1,0},{2,3},{3,2},{4,5},{5,4},{6,7},{7,6},{8,9},{9,8},{10,11... | collective-permute-start | bytes 1505288 | tf_op jit(solution)/shard_map/ppermute | solution.py:40
  48.9 5.3 %copy-start.4 = (bf16[56,2240]{1,0:T(8,128)(2,1)}, bf16[56,2240]{1,0:T(8,128)(2,1)S(1)}, u32[]{:S(2)}) copy-start(bf16[56,2240]{1,0:T(8,128)(2,1)S(1)} %collective-permute-done.7) | copy-start | bytes 752644
  49.9 11.3 %collective-permute-start.8 = (bf16[2,56,2240]{2,1,0:T(8,128)(2,1)}, bf16[2,56,2240]{2,1,0:T(8,128)(2,1)}, u32[]{:S(2)}, u32[]{:S(2)}) collective-permute-start(bf16[2,56,2240]{2,1,0:T(8,128)(2,1)} %pad_maximum_fusion.2), channel_id=1, source_target_pairs={{0,1},{1,0},{2,3},{3,2},{4,5},{5,4},{6,7},{7,6},{8,9},{9,8},{10,11... | collective-permute-start | bytes 1505288 | tf_op jit(solution)/shard_map/ppermute | solution.py:40
  54.2 8.9 %copy-start.2 = (bf16[512,2240]{0,1:T(8,128)(2,1)S(1)}, bf16[512,2240]{0,1:T(8,128)(2,1)}, u32[]{:S(2)}) copy-start(bf16[512,2240]{0,1:T(8,128)(2,1)} %param.9) | copy-start | bytes 6881284

commit v5 on v2

--- a/solution.py
+++ b/solution.py
@@ -37,8 +37,11 @@
             lax.ppermute(piece, "groups", [(a, (a + s) % ng) for a in range(ng)])
             for s in range(1, ng)
         ]
-        from_core = lax.ppermute(jnp.stack(from_groups), "heads", swap)
-        pieces += from_groups + [from_core[s] for s in range(ng)]
+        from_core = [lax.ppermute(piece, "heads", swap)]
+        if ng > 1:
+            rest = lax.ppermute(jnp.stack(from_groups[1:]), "heads", swap)
+            from_core += [rest[s] for s in range(ng - 1)]
+        pieces += from_groups + from_core
     return jnp.concatenate(pieces, axis=0), jnp.stack(shares)
 
 

time: 67.2 us -> 65.9 us (0.981)
  waiting for transfers between devices: 13 us -> 8.8 us
  local copies, waits for them, and re-layouts: 15.4 us -> 19.2 us
  other arithmetic: 8.46 us -> 7.73 us
    ppermute x3, waiting for transfers between devices: 10.1 us -> 3.06 us  [_ring_out_proj(): lax.ppermute(piece, 'groups', [(a, (a + s) % ng) for a in range(ng)])]
    unnamed x19 -> x21, local copies, waits for them, and re-layouts: 13 us -> 16.8 us
    ppermute x3, waiting for transfers between devices: 2.87 us -> 5.48 us  [_ring_out_proj(): piece = lax.ppermute(piece, 'frames', ring)]
    another operation x1, other arithmetic: 1.29 us -> 0.12 us  [_attend(): prefix_state = earlier_state[None] + jnp.cumsum(frame_state, axis=0)]
    another operation x4 -> x1, other arithmetic: 1.1 us -> 0.01 us  [the longest x3 1.09 us: _ring_out_proj(): from_core = lax.ppermute(jnp.stack(from_groups), 'heads', swap)]
    another operation x1, other arithmetic: 0.2 us -> 1.1 us  [_attend(): prefix_sum = earlier_sum[None] + jnp.cumsum(frame_sum, axis=0)]
  transfers between devices with their start and end apart: 11 -> 14, of which waited for: 3 -> 5; matrix products, arithmetic and copies ran while one was open for 40% -> 46% of each run, Pallas kernels for 0% -> 0%
where the time goes in v5:
time: 65.9 us; the launch traced here: 65.3 us
  local copies, waits for them, and re-layouts  19.2 us (29%)
  starting transfers between devices  16.6 us (25%)
  matrix products  12.8 us (19%)
  waiting for transfers between devices  8.8 us (13%)
  other arithmetic  7.73 us (12%)
    unnamed x21, local copies, waits for them, and re-layouts  16.8 us
    dot_general x1, matrix products, _project(): projected = jnp.dot(matched, weights, preferred_element_type=jnp.float32)  8.07 us
    ppermute x3, waiting for transfers between devices, _ring_out_proj(): piece = lax.ppermute(piece, 'frames', ring)  5.48 us
    ppermute x3, starting transfers between devices, _ring_out_proj(): piece = lax.ppermute(piece, 'frames', ring)  5.08 us
    all_to_all x1, starting transfers between devices, _exclusive_prefix(): lax.all_to_all(outgoing, 'frames', split_axis=0, concat_axis=0, tiled=True)  3.86 us
    ppermute x3, starting transfers between devices, _ring_out_proj(): lax.ppermute(piece, 'groups', [(a, (a + s) % ng) for a in range(ng)])  3.55 us
    all_to_all x1, starting transfers between devices, _project(): lax.all_to_all(attended, 'heads', split_axis=0, concat_axis=1, tiled=True)  3.51 us
    ppermute x3, waiting for transfers between devices, _ring_out_proj(): lax.ppermute(piece, 'groups', [(a, (a + s) % ng) for a in range(ng)])  3.06 us
  transfers between devices with their start and end apart: 14, of which 5 were waited for; matrix products, arithmetic and copies ran while one was open for 46% of the time, Pallas kernels for 0%

profile of v5, /device:TPU:0, one launch (start us, length us, event | category | flops | bytes accessed | tf_op | source)
XLA Modules:
  0.0 65.3 jit_solution(18389738736912680626)
XLA Ops:
  0.0 1.8 %constant_dynamic-update-slice_fusion.9 = (bf16[896,2240]{1,0:T(8,128)(2,1)}, bf16[56,2240]{1,0:T(8,128)(2,1)}) fusion(bf16[224,2240]{1,0:T(8,128)(2,1)} %param.10, s32[]{:T(128)S(6)} %select_n.85), kind=kLoop, calls=%fused_computation.51 | loop fusion | bytes 766980
  1.8 3.1 %collective-permute-start = (bf16[56,2240]{1,0:T(8,128)(2,1)}, bf16[56,2240]{1,0:T(8,128)(2,1)}, u32[]{:S(2)}, u32[]{:S(2)}) collective-permute-start(bf16[56,2240]{1,0:T(8,128)(2,1)} %get-tuple-element.6), channel_id=1, source_target_pairs={{0,4},{4,8},{8,12},{12,0},{1,5},{5,9},{9,13},{13,1},{2,6},{6,10},{... | collective-permute-start | bytes 752648 | tf_op jit(solution)/shard_map/ppermute | solution.py:35
  4.9 1.2 %broadcast_maximum_fusion = bf16[2048,224]{0,1:T(8,128)(2,1)S(1)} fusion(bf16[2048,224]{0,1:T(8,128)(2,1)} %param.7), kind=kLoop, calls=%fused_computation.23 | loop fusion | flops 458752 | bytes 1835008 | tf_op jit(solution)/shard_map/max | solution.py:63
  6.1 1.4 %convert_reduce_fusion.1 = f32[224]{0:T(256)S(1)} fusion(bf16[2048,224]{0,1:T(8,128)(2,1)} %param.7), kind=kLoop, calls=%fused_computation.7 | loop fusion | flops 1376032 | bytes 918400 | tf_op jit(solution)/shard_map/reduce_sum | solution.py:74
  7.6 2.6 %fusion.22 = (f32[224,224]{1,0:T(8,128)S(1)}, f32[4,224,224]{2,1,0:T(8,128)}) fusion(bf16[28,4,8,512]{3,2,1,0:T(8,128)(2,1)} %bitcast.55, bf16[28,4,8,512]{3,2,1,0:T(8,128)(2,1)S(1)} %bitcast.48, pred[224,224]{1,0:T(8,128)(4,1)S(1)} %broadcast_compare_fusion), kind=kOutput, calls=%fused_computation.69 | convolution fusion | flops 205872128 | bytes 2888704 | tf_op jit(solution)/shard_map/fti,ftj->fij/dot_general | solution.py:68
  10.5 0.9 %broadcast_select_fusion = f32[4,2,113,112]{2,3,1,0:T(8,128)} fusion(f32[2,113,112]{1,2,0:T(8,128)S(1)} %copy.41, pred[4]{0:T(512)(128)(4,1)S(1)} %iota_compare_fusion.6), kind=kLoop, calls=%fused_computation.35 | loop fusion | flops 101248 | bytes 506244 | tf_op jit(solution)/shard_map/jit(_where)/select_n | solution.py:16
  11.4 3.9 %all-to-all-start = ((f32[4,2,113,112]{2,3,1,0:T(8,128)}), f32[4,2,113,112]{2,3,1,0:T(8,128)S(1)}, u32[]{:S(2)}, u32[]{:S(2)}) async-start(f32[4,2,113,112]{2,3,1,0:T(8,128)} %broadcast_select_fusion), calls=%async_computation | async-start | bytes 917504 | tf_op jit(solution)/shard_map/all_to_all | solution.py:19
  16.4 1.2 %broadcast_maximum_fusion.1 = bf16[2048,224]{0,1:T(8,128)(2,1)S(1)} fusion(bf16[2048,224]{0,1:T(8,128)(2,1)} %param.6), kind=kLoop, calls=%fused_computation.24 | loop fusion | flops 458752 | bytes 1835008 | tf_op jit(solution)/shard_map/max | solution.py:62
  17.6 1.1 %convert_reduce_fusion = f32[4,224]{0,1:T(8,128)} fusion(bf16[4,512,224]{1,0,2:T(4,128)(2,1)S(1)} %reshape.148), kind=kLoop, calls=%fused_computation.6 | loop fusion | flops 916608 | bytes 921088 | tf_op jit(solution)/shard_map/reduce_sum | solution.py:72
  19.4 0.7 %dynamic-slice_dynamic-update-slice_fusion.1 = bf16[896,2240]{1,0:T(8,128)(2,1)} fusion(bf16[896,2240]{1,0:T(8,128)(2,1)} %dynamic-slice_dynamic-update-slice_fusion.2, bf16[224,2240]{1,0:T(8,128)(2,1)S(1)} %copy-done.1, s32[]{:T(128)S(6)} %select_n.87), kind=kLoop, calls=%fused_computation.30 | loop fusion | bytes 508932
  20.2 1.1 %reduce_window_sum.23 = f32[4,224]{0,1:T(8,128)S(1)} reduce-window(f32[4,224]{0,1:T(8,128)} %convert_reduce_fusion, f32[]{:T(128)} %constant.89.clone.1), window={size=4x1 pad=3_0x0_0}, to_apply=%region_5.6 | reduce-window | flops 2688 | bytes 7172 | tf_op jit(solution)/shard_map/jit(cumsum)/reduce_window_sum | solution.py:90
  21.3 0.7 %dynamic-slice_dynamic-update-slice_fusion = bf16[896,2240]{1,0:T(8,128)(2,1)} fusion(bf16[896,2240]{1,0:T(8,128)(2,1)} %dynamic-slice_dynamic-update-slice_fusion.1, bf16[224,2240]{1,0:T(8,128)(2,1)S(1)} %copy-done.1, s32[]{:T(128)S(6)} %select_n.88), kind=kLoop, calls=%fused_computation.29 | loop fusion | bytes 508932
  22.0 1.5 %collective-permute-start.1 = (bf16[56,2240]{1,0:T(8,128)(2,1)}, bf16[56,2240]{1,0:T(8,128)(2,1)}, u32[]{:S(2)}, u32[]{:S(2)}) collective-permute-start(bf16[56,2240]{1,0:T(8,128)(2,1)} %collective-permute-done), channel_id=1, source_target_pairs={{0,16},{16,0},{1,17},{17,1},{2,18},{18,2},{3,19},{19,3},{4,20},{20... | collective-permute-start | bytes 752648 | tf_op jit(solution)/shard_map/ppermute | solution.py:37
  23.6 2.0 %collective-permute-start.4 = (bf16[56,2240]{1,0:T(8,128)(2,1)}, bf16[56,2240]{1,0:T(8,128)(2,1)S(1)}, u32[]{:S(2)}, u32[]{:S(2)}) collective-permute-start(bf16[56,2240]{1,0:T(8,128)(2,1)} %collective-permute-done), channel_id=1, source_target_pairs={{0,4},{4,8},{8,12},{12,0},{1,5},{5,9},{9,13},{13,1},{2,6},{6,10},{... | collective-permute-start | bytes 752648 | tf_op jit(solution)/shard_map/ppermute | solution.py:35
  25.6 1.7 %constant_dynamic-update-slice_fusion.8 = bf16[896,2240]{1,0:T(8,128)(2,1)} fusion(bf16[896,2240]{1,0:T(8,128)(2,1)} %dynamic-slice_dynamic-update-slice_fusion, bf16[56,2240]{1,0:T(8,128)(2,1)} %collective-permute-done), kind=kLoop, calls=%fused_computation.50 | loop fusion | bytes 516096
  27.3 2.4 %collective-permute-done.1 = bf16[56,2240]{1,0:T(8,128)(2,1)} collective-permute-done((bf16[56,2240]{1,0:T(8,128)(2,1)}, bf16[56,2240]{1,0:T(8,128)(2,1)}, u32[]{:S(2)}, u32[]{:S(2)}) %collective-permute-start.1) | collective-permute-done | bytes 250912 | tf_op jit(solution)/shard_map/ppermute | solution.py:37
  29.8 4.7 %collective-permute-done.4 = bf16[56,2240]{1,0:T(8,128)(2,1)S(1)} collective-permute-done((bf16[56,2240]{1,0:T(8,128)(2,1)}, bf16[56,2240]{1,0:T(8,128)(2,1)S(1)}, u32[]{:S(2)}, u32[]{:S(2)}) %collective-permute-start.4) | collective-permute-done | bytes 250912 | tf_op jit(solution)/shard_map/ppermute | solution.py:35
  35.1 1.7 %constant_dynamic-update-slice_fusion.7 = bf16[896,2240]{1,0:T(8,128)(2,1)} fusion(bf16[896,2240]{1,0:T(8,128)(2,1)} %constant_dynamic-update-slice_fusion.8, bf16[56,2240]{1,0:T(8,128)(2,1)} %collective-permute-done.1), kind=kLoop, calls=%fused_computation.49 | loop fusion | bytes 516096
  36.8 0.7 %constant_dynamic-update-slice_fusion.6 = bf16[896,2240]{1,0:T(8,128)(2,1)} fusion(bf16[896,2240]{1,0:T(8,128)(2,1)} %constant_dynamic-update-slice_fusion.7, bf16[56,2240]{1,0:T(8,128)(2,1)S(1)} %collective-permute-done.2), kind=kLoop, calls=%fused_computation.48 | loop fusion | bytes 508928
  39.1 1.6 %divide_convert_fusion = bf16[4,512,224]{1,2,0:T(8,128)(2,1)} fusion(f32[4,512,224]{1,2,0:T(8,128)S(1)} %fusion.11, bf16[28,4,8,512]{3,2,1,0:T(8,128)(2,1)S(1)} %bitcast.50, pred[224,224]{1,0:T(8,128)(4,1)S(1)} %broadcast_compare_fusion, bf16[4,224]{1,0:T(4,128)(2,1)S(1)} %copy.45), kind=kOutput, calls=%fused_computation.5 | convolution fusion | flops 207097856 | bytes 3721984 | tf_op jit(solution)/shard_map/fti,fij->ftj/dot_general | solution.py:98
  40.7 3.5 %all-to-all-start.1 = ((bf16[4,512,224]{1,2,0:T(8,128)(2,1)}), bf16[4,512,224]{1,2,0:T(8,128)(2,1)S(1)}, u32[]{:S(2)}, u32[]{:S(2)}) async-start(bf16[4,512,224]{1,2,0:T(8,128)(2,1)} %divide_convert_fusion), calls=%async_computation.1 | async-start | bytes 1835008 | tf_op jit(solution)/shard_map/all_to_all | solution.py:114
  44.8 0.8 %collective-permute-done.8 = bf16[56,2240]{1,0:T(8,128)(2,1)S(1)} collective-permute-done((bf16[56,2240]{1,0:T(8,128)(2,1)S(1)}, bf16[56,2240]{1,0:T(8,128)(2,1)S(1)}, u32[]{:S(2)}, u32[]{:S(2)}) %collective-permute-start.8) | collective-permute-done | bytes 250912 | tf_op jit(solution)/shard_map/ppermute | solution.py:35
  45.5 1.4 %collective-permute-start.9 = (bf16[56,2240]{1,0:T(8,128)(2,1)S(1)}, bf16[56,2240]{1,0:T(8,128)(2,1)S(1)}, u32[]{:S(2)}, u32[]{:S(2)}) collective-permute-start(bf16[56,2240]{1,0:T(8,128)(2,1)S(1)} %collective-permute-done.8), channel_id=1, source_target_pairs={{0,16},{16,0},{1,17},{17,1},{2,18},{18,2},{3,19},{19,3},{4,20},{20... | collective-permute-start | bytes 752648 | tf_op jit(solution)/shard_map/ppermute | solution.py:37
  46.9 1.7 %bitcast_dynamic-update-slice_fusion.2 = bf16[896,2240]{1,0:T(8,128)(2,1)} fusion(bf16[896,2240]{1,0:T(8,128)(2,1)} %constant_dynamic-update-slice_fusion.6, bf16[1,56,2240]{2,1,0:T(8,128)(2,1)} %collective-permute-done.3), kind=kLoop, calls=%fused_computation.28 | loop fusion | bytes 516096
  48.6 0.7 %constant_dynamic-update-slice_fusion.5 = bf16[896,2240]{1,0:T(8,128)(2,1)} fusion(bf16[896,2240]{1,0:T(8,128)(2,1)} %bitcast_dynamic-update-slice_fusion.2, bf16[56,2240]{1,0:T(8,128)(2,1)S(1)} %collective-permute-done.4), kind=kLoop, calls=%fused_computation.47 | loop fusion | bytes 508928
  49.4 1.7 %constant_dynamic-update-slice_fusion.4 = bf16[896,2240]{1,0:T(8,128)(2,1)} fusion(bf16[896,2240]{1,0:T(8,128)(2,1)} %constant_dynamic-update-slice_fusion.5, bf16[56,2240]{1,0:T(8,128)(2,1)} %collective-permute-done.5), kind=kLoop, calls=%fused_computation.46 | loop fusion | bytes 516096
  51.0 1.7 %constant_dynamic-update-slice_fusion.3 = bf16[896,2240]{1,0:T(8,128)(2,1)} fusion(bf16[896,2240]{1,0:T(8,128)(2,1)} %constant_dynamic-update-slice_fusion.4, bf16[56,2240]{1,0:T(8,128)(2,1)} %collective-permute-done.6), kind=kLoop, calls=%fused_computation.45 | loop fusion | bytes 516096
  53.3 0.7 %bitcast_dynamic-update-slice_fusion.1 = bf16[896,2240]{1,0:T(8,128)(2,1)} fusion(bf16[896,2240]{1,0:T(8,128)(2,1)} %constant_dynamic-update-slice_fusion.3, bf16[1,56,2240]{2,1,0:T(8,128)(2,1)S(1)} %collective-permute-done.7), kind=kLoop, calls=%fused_computation.27 | loop fusion | bytes 508928
  54.0 0.7 %constant_dynamic-update-slice_fusion.2 = bf16[896,2240]{1,0:T(8,128)(2,1)} fusion(bf16[896,2240]{1,0:T(8,128)(2,1)} %bitcast_dynamic-update-slice_fusion.1, bf16[56,2240]{1,0:T(8,128)(2,1)S(1)} %collective-permute-done.8), kind=kLoop, calls=%fused_computation.44 | loop fusion | bytes 508928
  54.8 0.7 %constant_dynamic-update-slice_fusion.1 = bf16[896,2240]{1,0:T(8,128)(2,1)} fusion(bf16[896,2240]{1,0:T(8,128)(2,1)} %constant_dynamic-update-slice_fusion.2, bf16[56,2240]{1,0:T(8,128)(2,1)S(1)} %collective-permute-done.9), kind=kLoop, calls=%fused_computation.43 | loop fusion | bytes 508928
  55.5 0.7 %constant_dynamic-update-slice_fusion = bf16[896,2240]{1,0:T(8,128)(2,1)} fusion(bf16[896,2240]{1,0:T(8,128)(2,1)} %constant_dynamic-update-slice_fusion.1, bf16[56,2240]{1,0:T(8,128)(2,1)S(1)} %collective-permute-done.10), kind=kLoop, calls=%fused_computation.42 | loop fusion | bytes 508928
  57.2 8.1 %fusion.1 = bf16[512,2240]{0,1:T(8,128)(2,1)} fusion(bf16[896,2240]{1,0:T(8,128)(2,1)} %bitcast_dynamic-update-slice_fusion, bf16[512,2240]{0,1:T(8,128)(2,1)} %param.9, f32[2240]{0:T(1024)S(1)} %dynamic-slice_reduce_fusion, bf16[512,896]{0,1:T(8,128)(2,1)S(1)} %bitcast.52, s32[896]{0:T(1024)S(1)} %add.155), kind=kOutput, calls=%fused_computation.2 | convolution fusion | flops 2883141632 | bytes 9531648 | tf_op jit(solution)/shard_map/dot_general | solution.py:124
  (53 shorter events, 6.5 us)
Async XLA Ops:
  0.0 20.1 %copy-start = (f32[4,2240]{1,0:T(4,128)S(1)}, f32[4,2240]{1,0:T(4,128)}, u32[]{:S(2)}) copy-start(f32[4,2240]{1,0:T(4,128)} %param.11) | copy-start | bytes 107524
  1.8 20.2 %collective-permute-start = (bf16[56,2240]{1,0:T(8,128)(2,1)}, bf16[56,2240]{1,0:T(8,128)(2,1)}, u32[]{:S(2)}, u32[]{:S(2)}) collective-permute-start(bf16[56,2240]{1,0:T(8,128)(2,1)} %get-tuple-element.6), channel_id=1, source_target_pairs={{0,4},{4,8},{8,12},{12,0},{1,5},{5,9},{9,13},{13,1},{2,6},{6,10},{... | collective-permute-start | bytes 752648 | tf_op jit(solution)/shard_map/ppermute | solution.py:35
  10.2 8.5 %copy-start.1 = (bf16[224,2240]{1,0:T(8,128)(2,1)S(1)}, bf16[224,2240]{1,0:T(8,128)(2,1)}, u32[]{:S(2)}) copy-start(bf16[224,2240]{1,0:T(8,128)(2,1)} %param.10) | copy-start | bytes 3010564
  11.4 26.1 %all-to-all-start = ((f32[4,2,113,112]{2,3,1,0:T(8,128)}), f32[4,2,113,112]{2,3,1,0:T(8,128)S(1)}, u32[]{:S(2)}, u32[]{:S(2)}) async-start(f32[4,2,113,112]{2,3,1,0:T(8,128)} %broadcast_select_fusion), calls=%async_computation | async-start | bytes 917504 | tf_op jit(solution)/shard_map/all_to_all | solution.py:19
  18.7 19.7 %copy-start.2 = (f32[4,224,224]{2,1,0:T(8,128)S(1)}, f32[4,224,224]{2,1,0:T(8,128)}, u32[]{:S(2)}) copy-start(f32[4,224,224]{2,1,0:T(8,128)} %get-tuple-element.10) | copy-start | bytes 2408452
  22.0 7.7 %collective-permute-start.1 = (bf16[56,2240]{1,0:T(8,128)(2,1)}, bf16[56,2240]{1,0:T(8,128)(2,1)}, u32[]{:S(2)}, u32[]{:S(2)}) collective-permute-start(bf16[56,2240]{1,0:T(8,128)(2,1)} %collective-permute-done), channel_id=1, source_target_pairs={{0,16},{16,0},{1,17},{17,1},{2,18},{18,2},{3,19},{19,3},{4,20},{20... | collective-permute-start | bytes 752648 | tf_op jit(solution)/shard_map/ppermute | solution.py:37
  23.6 13.2 %collective-permute-start.2 = (bf16[56,2240]{1,0:T(8,128)(2,1)}, bf16[56,2240]{1,0:T(8,128)(2,1)S(1)}, u32[]{:S(2)}, u32[]{:S(2)}) collective-permute-start(bf16[56,2240]{1,0:T(8,128)(2,1)} %collective-permute-done), channel_id=1, source_target_pairs={{0,1},{1,0},{2,3},{3,2},{4,5},{5,4},{6,7},{7,6},{8,9},{9,8},{10,11... | collective-permute-start | bytes 752648 | tf_op jit(solution)/shard_map/ppermute | solution.py:40
  23.6 10.9 %collective-permute-start.4 = (bf16[56,2240]{1,0:T(8,128)(2,1)}, bf16[56,2240]{1,0:T(8,128)(2,1)S(1)}, u32[]{:S(2)}, u32[]{:S(2)}) collective-permute-start(bf16[56,2240]{1,0:T(8,128)(2,1)} %collective-permute-done), channel_id=1, source_target_pairs={{0,4},{4,8},{8,12},{12,0},{1,5},{5,9},{9,13},{13,1},{2,6},{6,10},{... | collective-permute-start | bytes 752648 | tf_op jit(solution)/shard_map/ppermute | solution.py:35
  29.7 17.2 %collective-permute-start.3 = (bf16[1,56,2240]{2,1,0:T(8,128)(2,1)}, bf16[1,56,2240]{2,1,0:T(8,128)(2,1)}, u32[]{:S(2)}, u32[]{:S(2)}) collective-permute-start(bf16[1,56,2240]{2,1,0:T(8,128)(2,1)} %bitcast.10), channel_id=1, source_target_pairs={{0,1},{1,0},{2,3},{3,2},{4,5},{5,4},{6,7},{7,6},{8,9},{9,8},{10,11... | collective-permute-start | bytes 752648 | tf_op jit(solution)/shard_map/ppermute | solution.py:42
  34.5 9.7 %collective-permute-start.5 = (bf16[56,2240]{1,0:T(8,128)(2,1)S(1)}, bf16[56,2240]{1,0:T(8,128)(2,1)}, u32[]{:S(2)}, u32[]{:S(2)}) collective-permute-start(bf16[56,2240]{1,0:T(8,128)(2,1)S(1)} %collective-permute-done.4), channel_id=1, source_target_pairs={{0,16},{16,0},{1,17},{17,1},{2,18},{18,2},{3,19},{19,3},{4,20},{20... | collective-permute-start | bytes 752648 | tf_op jit(solution)/shard_map/ppermute | solution.py:37
  35.1 15.9 %collective-permute-start.6 = (bf16[56,2240]{1,0:T(8,128)(2,1)S(1)}, bf16[56,2240]{1,0:T(8,128)(2,1)}, u32[]{:S(2)}, u32[]{:S(2)}) collective-permute-start(bf16[56,2240]{1,0:T(8,128)(2,1)S(1)} %collective-permute-done.4), channel_id=1, source_target_pairs={{0,1},{1,0},{2,3},{3,2},{4,5},{5,4},{6,7},{7,6},{8,9},{9,8},{10,11... | collective-permute-start | bytes 752648 | tf_op jit(solution)/shard_map/ppermute | solution.py:40
  35.1 10.4 %collective-permute-start.8 = (bf16[56,2240]{1,0:T(8,128)(2,1)S(1)}, bf16[56,2240]{1,0:T(8,128)(2,1)S(1)}, u32[]{:S(2)}, u32[]{:S(2)}) collective-permute-start(bf16[56,2240]{1,0:T(8,128)(2,1)S(1)} %collective-permute-done.4), channel_id=1, source_target_pairs={{0,4},{4,8},{8,12},{12,0},{1,5},{5,9},{9,13},{13,1},{2,6},{6,10},{... | collective-permute-start | bytes 752648 | tf_op jit(solution)/shard_map/ppermute | solution.py:35
  40.7 16.5 %all-to-all-start.1 = ((bf16[4,512,224]{1,2,0:T(8,128)(2,1)}), bf16[4,512,224]{1,2,0:T(8,128)(2,1)S(1)}, u32[]{:S(2)}, u32[]{:S(2)}) async-start(bf16[4,512,224]{1,2,0:T(8,128)(2,1)} %divide_convert_fusion), calls=%async_computation.1 | async-start | bytes 1835008 | tf_op jit(solution)/shard_map/all_to_all | solution.py:114
  44.2 9.1 %collective-permute-start.7 = (bf16[1,56,2240]{2,1,0:T(8,128)(2,1)}, bf16[1,56,2240]{2,1,0:T(8,128)(2,1)S(1)}, u32[]{:S(2)}, u32[]{:S(2)}) collective-permute-start(bf16[1,56,2240]{2,1,0:T(8,128)(2,1)} %bitcast.12), channel_id=1, source_target_pairs={{0,1},{1,0},{2,3},{3,2},{4,5},{5,4},{6,7},{7,6},{8,9},{9,8},{10,11... | collective-permute-start | bytes 752648 | tf_op jit(solution)/shard_map/ppermute | solution.py:42
  45.5 7.8 %collective-permute-start.9 = (bf16[56,2240]{1,0:T(8,128)(2,1)S(1)}, bf16[56,2240]{1,0:T(8,128)(2,1)S(1)}, u32[]{:S(2)}, u32[]{:S(2)}) collective-permute-start(bf16[56,2240]{1,0:T(8,128)(2,1)S(1)} %collective-permute-done.8), channel_id=1, source_target_pairs={{0,16},{16,0},{1,17},{17,1},{2,18},{18,2},{3,19},{19,3},{4,20},{20... | collective-permute-start | bytes 752648 | tf_op jit(solution)/shard_map/ppermute | solution.py:37
  46.9 8.6 %collective-permute-start.10 = (bf16[56,2240]{1,0:T(8,128)(2,1)S(1)}, bf16[56,2240]{1,0:T(8,128)(2,1)S(1)}, u32[]{:S(2)}, u32[]{:S(2)}) collective-permute-start(bf16[56,2240]{1,0:T(8,128)(2,1)S(1)} %collective-permute-done.8), channel_id=1, source_target_pairs={{0,1},{1,0},{2,3},{3,2},{4,5},{5,4},{6,7},{7,6},{8,9},{9,8},{10,11... | collective-permute-start | bytes 752648 | tf_op jit(solution)/shard_map/ppermute | solution.py:40
  53.3 2.9 %collective-permute-start.11 = (bf16[1,56,2240]{2,1,0:T(8,128)(2,1)S(1)}, bf16[1,56,2240]{2,1,0:T(8,128)(2,1)S(1)}, u32[]{:S(2)}, u32[]{:S(2)}) collective-permute-start(bf16[1,56,2240]{2,1,0:T(8,128)(2,1)S(1)} %bitcast.53), channel_id=1, source_target_pairs={{0,1},{1,0},{2,3},{3,2},{4,5},{5,4},{6,7},{7,6},{8,9},{9,8},{10,11... | collective-permute-start | bytes 752648 | tf_op jit(solution)/shard_map/ppermute | solution.py:42
